TPU v7x, 256 devices: a whole 4x4x8 slice. The times are simulated.
256 devices in a mesh: ctx: 32 (over y, x, core), exp: 8 (over z).
Axes of the slice: x: 4, y: 4, z: 8, core: 2. Of those that a mesh axis runs over, the one named last changes fastest.
Arguments:
- ssm_input: bfloat16 [4096, 4096], P('ctx', 'exp'), may hold values from -6 to 6
- gate_input: bfloat16 [4096, 4096], P('ctx', 'exp'), may hold values from -6 to 6
- key_proj: bfloat16 [4096, 128], P('ctx'), may hold values from -4 to 4
- query_proj: bfloat16 [4096, 128], P('ctx'), may hold values from -4 to 4
- step_size: float32 [4096, 64], P('ctx', 'exp'), may hold values from 0 to 1, as said below
- decay_rate: float32 [64], P('exp'), may hold values from 0.5 to 1.5
- head_gain: float32 [4096], P('exp'), may hold values from 0.5 to 1.5
- residual: bfloat16 [4096, 4096], P('ctx', 'exp'), may hold values from -33 to 33
- ffn_gain: float32 [4096], replicated, may hold values from 0.5 to 1.5
- gate_weight: bfloat16 [8, 4096, 12288], P('exp', None, 'ctx'), may hold values from -0.09375 to 0.09375
- up_weight: bfloat16 [8, 4096, 12288], P('exp', None, 'ctx'), may hold values from -0.09375 to 0.09375
- down_weight: bfloat16 [8, 12288, 4096], P('exp', 'ctx'), may hold values from -0.0546875 to 0.0546875
- expert_ids: int32 [4096, 2], P('ctx'), may hold values from 0 to 7, all different within a row; in each aligned block of 128 rows (0 to 127, 128 to 255, ...) at most 48 rows name the same one
- route_weight: float32 [4096, 2], P('ctx'), may hold values from 0.5 to 2
Outputs:
- block_out: bfloat16 [4096, 4096], P('ctx', 'exp')
- expert_out: bfloat16 [4096, 4096], P('ctx', 'exp')
Inputs may be any that keep to these rules, and one draw needn't show every extreme that they name: `step_size`: step sizes are positive. `expert_ids`: the two experts of a token differ. In each aligned block of 128 rows (the tokens of one shard) no expert is named by more than 48 rows, and in some block one expert is named by exactly 48 rows.
All inputs are finite; a program needn't handle non-finite values.
Results may differ from a plain program's by a relative error of at most 0.022.
Values may be sent and summed in bfloat16 or wider, within the bound.
No kernel may reach another device: no remote copies, remote signals or barrier semaphores. Data moves between devices by JAX's collectives and lax.ppermute only.
A program may use at most 128 MiB of HBM per device.

v0:
```python
import jax
import jax.numpy as jnp
from jax import lax
from jax.sharding import PartitionSpec as P

precise = lax.Precision.HIGHEST


def carried_in(shard, axis, combine, identity):
    length, mine = (lax.axis_size(axis), lax.axis_index(axis))
    everything = jax.tree.map(
        lambda part, kind: lax.all_gather(part.astype(kind), axis),
        shard,
        (jnp.bfloat16, jnp.bfloat16),
    )
    start = jax.tree.map(
        lambda part, zero: jnp.broadcast_to(jnp.asarray(zero, part.dtype), part.shape),
        shard,
        identity,
    )

    def lap(k, before):
        reached = k < mine
        new = combine(
            before, jax.tree.map(lambda part, own: part[k].astype(own.dtype), everything, shard)
        )
        return jax.tree.map(lambda a, b: jnp.where(reached, a, b), new, before)

    return lax.fori_loop(0, length, lap, start)


def local_block(ssm_piece, key_piece, query_piece, step_piece, decay_rate, head_count):
    row_count = ssm_piece.shape[0]
    head_width = ssm_piece.shape[1] // head_count
    values = ssm_piece.astype(jnp.float32).reshape(row_count, head_count, head_width)
    key_vals = key_piece.astype(jnp.float32)
    queries = query_piece.astype(jnp.float32)
    log_steps = -step_piece * decay_rate[None, :]
    running = jnp.cumsum(log_steps, axis=0)
    scores = jnp.dot(queries, key_vals.T, precision=precise)
    causal = (jnp.arange(row_count)[:, None] >= jnp.arange(row_count)[None, :])[:, :, None]
    spacing = running[:, None, :] - running[None, :, :]
    decays = jnp.where(causal, jnp.exp(jnp.where(causal, spacing, 0.0)), 0.0)
    within = jnp.einsum("tsh,ts,shp->thp", decays, scores, values, precision=precise)
    overall = running[-1]
    fading = jnp.exp(overall[None, :] - running)
    states = jnp.einsum("sh,shp,sn->hpn", fading, values, key_vals, precision=precise)
    return (within, running, overall, states)


def route_tables(expert_ids, route_weight, experts, capacity):
    matched = expert_ids[None, :, :] == experts[:, None, None]
    member = jnp.any(matched, axis=2).astype(jnp.int32)
    gate_sum = jnp.sum(jnp.where(matched, route_weight[None, :, :], 0.0), axis=2)
    slot_index = jnp.cumsum(member, axis=1) - 1
    positions = jnp.arange(capacity, dtype=jnp.int32)
    routing = (
        (slot_index[:, None, :] == positions[None, :, None]) & (member[:, None, :] > 0)
    ).astype(jnp.float32)
    slot_weight = jnp.einsum("nkt,nt->nk", routing, gate_sum, precision=precise)
    return (routing, slot_weight)


def join_states(earlier, later):
    return (earlier[0] + later[0], jnp.exp(later[0])[:, None, None] * earlier[1] + later[1])


def on_device(
    ssm_input,
    gate_input,
    key_proj,
    query_proj,
    step_size,
    decay_rate,
    head_gain,
    residual,
    ffn_gain,
    gate_weight,
    up_weight,
    down_weight,
    expert_ids,
    route_weight,
):
    head_count = step_size.shape[1]
    row_count, channels = ssm_input.shape
    head_width = channels // head_count
    within, running, overall, states = local_block(
        ssm_input, key_proj, query_proj, step_size, decay_rate, head_count
    )
    prefix = carried_in(
        (overall, states), "ctx", join_states, (jnp.zeros_like(overall), jnp.zeros_like(states))
    )
    before = prefix[1]
    carried = jnp.einsum(
        "th,hpn,tn->thp",
        jnp.exp(running),
        before,
        query_proj.astype(jnp.float32),
        precision=precise,
    )
    mixer_out = within + carried
    gated_out = mixer_out * jax.nn.silu(gate_input.astype(jnp.float32)).reshape(
        row_count, head_count, head_width
    )
    inv_rms = lax.rsqrt(jnp.mean(gated_out * gated_out, axis=2, keepdims=True) + 1e-05)
    normed = (gated_out * inv_rms).reshape(row_count, channels) * head_gain[None, :]
    block_out = (residual.astype(jnp.float32) + normed).astype(jnp.bfloat16)
    owner_index = lax.axis_index("exp")
    exp_count = lax.axis_size("exp")
    capacity = 3 * row_count // exp_count
    tables, weights_all = route_tables(
        expert_ids, route_weight, jnp.arange(exp_count, dtype=jnp.int32), capacity
    )
    own_table = lax.dynamic_index_in_dim(tables, owner_index, 0, keepdims=False)
    own_weight = lax.dynamic_index_in_dim(weights_all, owner_index, 0, keepdims=False)
    gathered = lax.all_gather(block_out, "exp", axis=1, tiled=True)
    widened = gathered.astype(jnp.float32)
    ffn_input = (
        widened
        * lax.rsqrt(jnp.mean(widened * widened, axis=1, keepdims=True) + 1e-06)
        * ffn_gain[None, :]
    ).astype(jnp.bfloat16)
    chosen = jnp.dot(
        own_table.astype(jnp.bfloat16), ffn_input, preferred_element_type=jnp.float32
    ).astype(jnp.bfloat16)
    gate_here = gate_weight[0]
    up_here = up_weight[0]
    down_here = down_weight[0]
    token_piece = lax.all_gather(chosen, "ctx", axis=0, tiled=True)
    gate_proj = jnp.dot(token_piece, gate_here, preferred_element_type=jnp.float32)
    up_proj = jnp.dot(token_piece, up_here, preferred_element_type=jnp.float32)
    hidden = (jax.nn.silu(gate_proj) * up_proj).astype(jnp.bfloat16)
    summed = lax.psum_scatter(
        jnp.dot(hidden, down_here, preferred_element_type=jnp.float32).astype(jnp.bfloat16),
        "ctx",
        scatter_dimension=0,
        tiled=True,
    )
    spread = jnp.dot(
        own_table.T, own_weight[:, None] * summed.astype(jnp.float32), precision=precise
    )
    expert_out = lax.psum_scatter(
        spread.astype(jnp.bfloat16), "exp", scatter_dimension=1, tiled=True
    )
    return (block_out, expert_out)


def solution(mesh):
    placed = (
        P("ctx", "exp"),
        P("ctx", "exp"),
        P("ctx", None),
        P("ctx", None),
        P("ctx", "exp"),
        P("exp"),
        P("exp"),
        P("ctx", "exp"),
        P(),
        P("exp", None, "ctx"),
        P("exp", None, "ctx"),
        P("exp", "ctx", None),
        P("ctx", None),
        P("ctx", None),
    )
    return jax.shard_map(
        on_device,
        mesh=mesh,
        in_specs=placed,
        out_specs=(P("ctx", "exp"), P("ctx", "exp")),
        check_vma=False,
    )
```

profile of v0, /device:TPU:2, one launch (start us, length us, event | category | flops | bytes accessed | tf_op | source)
XLA Modules:
  0.0 405.1 jit_solution(16318344379442239635)
XLA Ops:
  9.1 1.0 copy.54
  10.2 1.7 convolution_convert_fusion.3
  12.7 21.7 %all-gather.1 = bf16[32,1,8]{2,1,0:T(2,128)(2,1)S(1)} all-gather(bf16[1,1,8]{2,1,0:T(2,128)(2,1)S(1)} %convert_bitcast_fusion), channel_id=1, replica_groups=mesh['ctx'=32,'exp'=8] {'ctx'}, dimensions={0}, use_global_device_ids=true | all-gather | bytes 528 | tf_op jit(solution)/shard_map/all_gather | solution.py:12
  35.2 1.7 convert_multiply_fusion.2
  36.9 1.8 copy.59
  39.3 1.6 fusion.52
  40.8 24.9 %all-gather.10.cloned.1.call-done = bf16[256,64,128]{2,1,0:T(8,128)(2,1)} async-done(((bf16[8,64,128]{2,1,0:T(8,128)(2,1)}), bf16[256,64,128]{2,1,0:T(8,128)(2,1)}) %all-gather.10.cloned.1.call-update) | async-done | bytes 4194320 | tf_op jit(solution)/shard_map/all_gather | solution.py:12
  65.8 33.8 %while.14 = (s32[]{:T(128)}, f32[8,64,128]{2,1,0:T(8,128)S(1)}, s32[]{:T(128)}, bf16[32,8]{1,0:T(8,128)(2,1)S(1)}, bf16[32,8,64,128]{3,2,1,0:T(8,128)(2,1)}, /*index=5*/s32[]{:T(128)}, s32[]{:T(128)}) while((s32[]{:T(128)}, f32[8,64,128]{2,1,0:T(8,128)S(1)}, s32[]{:T(128)}, bf16[32,8]{1,0:T(8,128)(2,1)S(1)}, ...), condition=%wide.region_2.3_spmd.clone, body=%wide.region_1.2_spmd.clone.sunk | while | flops 327692 | bytes 655545 | solution.py:29
  65.8 1.0 fusion.63
  66.8 1.0 fusion.63
  67.9 1.0 fusion.63
  68.9 1.0 fusion.63
  70.0 1.0 fusion.63
  71.0 1.0 fusion.63
  72.1 1.0 fusion.63
  73.2 1.0 fusion.63
  74.2 1.0 fusion.63
  75.3 1.0 fusion.63
  76.3 1.0 fusion.63
  77.4 1.0 fusion.63
  78.4 1.0 fusion.63
  79.5 1.0 fusion.63
  80.5 1.0 fusion.63
  81.6 1.0 fusion.63
  82.7 1.0 fusion.63
  83.7 1.0 fusion.63
  84.8 1.0 fusion.63
  85.8 1.0 fusion.63
  86.9 1.0 fusion.63
  89.0 1.0 fusion.63
  91.1 1.0 fusion.63
  92.2 1.0 fusion.63
  93.2 1.0 fusion.63
  94.3 1.0 fusion.63
  96.4 1.0 fusion.63
  98.5 1.0 fusion.63
  99.5 1.0 fusion.16
  100.6 1.8 multiply_reduce_fusion
  103.3 1.7 add_convert_fusion
  105.4 37.9 %all-gather.6.cloned.1.call-done = bf16[128,4096]{1,0:T(8,128)(2,1)} async-done(((bf16[128,512]{1,0:T(8,128)(2,1)}), bf16[128,4096]{1,0:T(8,128)(2,1)}) %all-gather.6.cloned.1.call-update) | async-done | bytes 1048592 | tf_op jit(solution)/shard_map/all_gather | solution.py:116
  143.4 1.5 fusion.10
  144.9 2.5 convolution_convert_fusion.2
  147.5 66.3 %all-gather.8.cloned.1.call-done = bf16[1536,4096]{1,0:T(8,128)(2,1)} async-done(((bf16[48,4096]{1,0:T(8,128)(2,1)}), bf16[1536,4096]{1,0:T(8,128)(2,1)}) %all-gather.8.cloned.1.call-update) | async-done | bytes 12582928 | tf_op jit(solution)/shard_map/all_gather | solution.py:129
  213.8 11.5 %fusion.3 = f32[1536,384]{1,0:T(8,128)} fusion(bf16[1536,4096]{1,0:T(8,128)(2,1)} %all-gather.8.cloned.1.call-done, bf16[1,4096,384]{2,1,0:T(8,128)(2,1)} %param.25), kind=kOutput, calls=%fused_computation.9 | convolution fusion | flops 4831838208 | bytes 18087936 | tf_op jit(solution)/shard_map/dot_general | solution.py:130
  225.3 20.0 %convolution_convert_fusion = bf16[1536,4096]{1,0:T(8,128)(2,1)} fusion(bf16[1,384,4096]{2,1,0:T(8,128)(2,1)S(1)} %copy-done, bf16[1536,4096]{1,0:T(8,128)(2,1)} %all-gather.8.cloned.1.call-done, bf16[1,4096,384]{2,1,0:T(8,128)(2,1)} %param.26, f32[1536,384]{1,0:T(8,128)} %fusion.3), kind=kOutput, calls=%fused_computation.3 | convolution fusion | flops 9673506816 | bytes 33816576 | tf_op jit(solution)/shard_map/dot_general | solution.py:134
  246.3 110.3 %reduce-scatter.3.cloned.1.call-done = bf16[48,4096]{1,0:T(8,128)(2,1)} async-done(((bf16[1536,4096]{1,0:T(8,128)(2,1)}), bf16[48,4096]{1,0:T(8,128)(2,1)}) %reduce-scatter.3.cloned.1.call-update) | async-done | bytes 393232 | tf_op jit(solution)/shard_map/reduce_scatter | solution.py:133
  356.5 3.0 convolution_convert_fusion.1
  359.6 39.0 %reduce-scatter.5.cloned.1.call-done = bf16[128,512]{1,0:T(8,128)(2,1)} async-done(((bf16[128,4096]{1,0:T(8,128)(2,1)}), bf16[128,512]{1,0:T(8,128)(2,1)}) %reduce-scatter.5.cloned.1.call-update) | async-done | bytes 131088 | tf_op jit(solution)/shard_map/reduce_scatter | solution.py:142
  (80 shorter events, 10.9 us)
Async XLA Ops:
  7.2 218.2 %copy-start = (bf16[1,384,4096]{2,1,0:T(8,128)(2,1)S(1)}, bf16[1,384,4096]{2,1,0:T(8,128)(2,1)}, u32[]{:S(2)}) copy-start(bf16[1,384,4096]{2,1,0:T(8,128)(2,1)} %param.27) | copy-start | bytes 9437188
  7.2 58.6 %all-gather.10.cloned.1.call-start = ((), (), s32[]{:S(2)}) async-start(), calls=%async_computation.6 | async-start | bytes 4325376 | tf_op jit(solution)/shard_map/all_gather | solution.py:12
  10.2 1.8 copy-start.1
  11.9 131.4 %all-gather.6.cloned.1.call-start = ((), (), s32[]{:S(2)}) async-start(), calls=%async_computation.2 | async-start | bytes 1179648 | tf_op jit(solution)/shard_map/all_gather | solution.py:116
  12.7 87.9 %copy-start.2 = (bf16[128,512]{0,1:T(8,128)(2,1)S(1)}, bf16[128,512]{0,1:T(8,128)(2,1)}, u32[]{:S(2)}) copy-start(bf16[128,512]{0,1:T(8,128)(2,1)} %copy-done.1) | copy-start | bytes 393220
  99.5 5.5 %copy-start.3 = (s32[128,2]{0,1:T(2,128)S(1)}, s32[128,2]{0,1:T(2,128)}, u32[]{:S(2)}) copy-start(s32[128,2]{0,1:T(2,128)} %param.28) | copy-start | bytes 3076
  105.0 108.8 %all-gather.8.cloned.1.call-start = ((), (), s32[]{:S(2)}) async-start(), calls=%async_computation.3 | async-start | bytes 12976128 | tf_op jit(solution)/shard_map/all_gather | solution.py:129
  147.4 209.1 %reduce-scatter.3.cloned.1.call-start = ((), (), s32[]{:S(2)}) async-start(), calls=%async_computation.4 | async-start | bytes 12976128 | tf_op jit(solution)/shard_map/reduce_scatter | solution.py:133
  245.3 0.7 copy-start.4
  245.4 153.2 %reduce-scatter.5.cloned.1.call-start = ((), (), s32[]{:S(2)}) async-start(), calls=%async_computation.5 | async-start | bytes 1179648 | tf_op jit(solution)/shard_map/reduce_scatter | solution.py:142
Sparse Core Ops, SparseCore 0:
  12.0 53.6 all-gather.9
  105.1 38.1 all-gather.5
  147.5 66.2 all-gather.7
  245.5 111.0 reduce-scatter.2
  359.7 38.8 reduce-scatter.4
where the time goes:
time: 406 us; the launch traced here: 405 us
  waiting for transfers between devices  278 us (68%)
  matrix products  43.4 us (11%)
  other arithmetic  40.5 us (10%)
  blocking collectives  21.7 us (5%)
  between operations  13.9 us (3%)
  local copies, waits for them, and re-layouts  5.99 us (1%)
    reduce_scatter x1, waiting for transfers between devices, on_device(): lax.psum_scatter(jnp.dot(hidden, down_here, preferred_element_type=jnp.fl...  110 us
    all_gather x1, waiting for transfers between devices, on_device(): token_piece = lax.all_gather(chosen, 'ctx', axis=0, tiled=True)  66.3 us
    reduce_scatter x1, waiting for transfers between devices, on_device(): lax.psum_scatter(spread.astype(jnp.bfloat16), 'exp', scatter_dimension=1,...  39 us
    all_gather x1, waiting for transfers between devices, on_device(): gathered = lax.all_gather(block_out, 'exp', axis=1, tiled=True)  37.9 us
    select_n x32, other arithmetic, lap(): return jax.tree.map(lambda a, b: jnp.where(reached, a, b), new, before)  32.4 us
    all_gather x1, waiting for transfers between devices, carried_in(): lax.all_gather(part.astype(kind), axis)  24.9 us
    all_gather x1, blocking collectives, carried_in(): lax.all_gather(part.astype(kind), axis)  21.7 us
    dot_general x1, matrix products, on_device(): jnp.dot(hidden, down_here, preferred_element_type=jnp.float32)  20 us
  transfers between devices with their start and end apart: 5, of which 5 were waited for; matrix products, arithmetic and copies ran while one was open for 2% of the time, Pallas kernels for 0%

commit v1 on v0

v1 whole, which is shorter than its diff:
```python
import jax
import jax.numpy as jnp
from jax import lax
from jax.sharding import Mesh, PartitionSpec as P

precise = lax.Precision.HIGHEST
CTX = ("chip", "core")


def local_block(ssm_piece, key_piece, query_piece, step_piece, decay_rate, head_count):
    row_count = ssm_piece.shape[0]
    head_width = ssm_piece.shape[1] // head_count
    values = ssm_piece.astype(jnp.float32).reshape(row_count, head_count, head_width)
    key_vals = key_piece.astype(jnp.float32)
    queries = query_piece.astype(jnp.float32)
    log_steps = -step_piece * decay_rate[None, :]
    running = jnp.cumsum(log_steps, axis=0)
    scores = jnp.dot(queries, key_vals.T, precision=precise)
    causal = (jnp.arange(row_count)[:, None] >= jnp.arange(row_count)[None, :])[:, :, None]
    spacing = running[:, None, :] - running[None, :, :]
    decays = jnp.where(causal, jnp.exp(jnp.where(causal, spacing, 0.0)), 0.0)
    within = jnp.einsum("tsh,ts,shp->thp", decays, scores, values, precision=precise)
    overall = running[-1]
    fading = jnp.exp(overall[None, :] - running)
    states = jnp.einsum("sh,shp,sn->hpn", fading, values, key_vals, precision=precise)
    return (within, running, overall, states)


def route_tables(expert_ids, route_weight, experts, capacity):
    matched = expert_ids[None, :, :] == experts[:, None, None]
    member = jnp.any(matched, axis=2).astype(jnp.int32)
    gate_sum = jnp.sum(jnp.where(matched, route_weight[None, :, :], 0.0), axis=2)
    slot_index = jnp.cumsum(member, axis=1) - 1
    positions = jnp.arange(capacity, dtype=jnp.int32)
    routing = (
        (slot_index[:, None, :] == positions[None, :, None]) & (member[:, None, :] > 0)
    ).astype(jnp.float32)
    return (routing, gate_sum)


def carried_state(overall, states):
    head_count, head_width, nstate = states.shape
    flat = states.astype(jnp.bfloat16).reshape(head_count * head_width, nstate)
    high = overall.astype(jnp.bfloat16)
    low = (overall - high.astype(jnp.float32)).astype(jnp.bfloat16)
    extra = jnp.zeros((8, nstate), jnp.bfloat16)
    extra = extra.at[0, :head_count].set(high).at[1, :head_count].set(low)
    packed = jnp.concatenate([flat, extra], axis=0)
    chips = lax.axis_size("chip")
    cores = lax.axis_size("core")
    by_chip = lax.all_gather(packed, "chip")
    everything = lax.all_gather(by_chip, "core")
    shards = chips * cores
    everything = everything.reshape(shards, packed.shape[0], nstate)
    core_of = jnp.arange(shards, dtype=jnp.int32) // chips
    chip_of = jnp.arange(shards, dtype=jnp.int32) % chips
    shard_of = chip_of * cores + core_of
    me = lax.axis_index("chip") * cores + lax.axis_index("core")
    rows = head_count * head_width
    decay_all = (
        everything[:, rows, :head_count].astype(jnp.float32)
        + everything[:, rows + 1, :head_count].astype(jnp.float32)
    )
    between = (shard_of[:, None] < shard_of[None, :]) & (shard_of[None, :] < me)
    spans = jnp.sum(jnp.where(between[:, :, None], decay_all[None, :, :], 0.0), axis=1)
    weight = jnp.where((shard_of < me)[:, None], jnp.exp(spans), 0.0)
    gathered = everything[:, :rows, :].astype(jnp.float32).reshape(
        shards, head_count, head_width, nstate
    )
    return jnp.einsum("kh,khpn->hpn", weight, gathered, precision=precise)


def on_device(
    ssm_input,
    gate_input,
    key_proj,
    query_proj,
    step_size,
    decay_rate,
    head_gain,
    residual,
    ffn_gain,
    gate_weight,
    up_weight,
    down_weight,
    expert_ids,
    route_weight,
):
    head_count = step_size.shape[1]
    row_count, channels = ssm_input.shape
    head_width = channels // head_count
    within, running, overall, states = local_block(
        ssm_input, key_proj, query_proj, step_size, decay_rate, head_count
    )
    before = carried_state(overall, states)
    carried = jnp.einsum(
        "th,hpn,tn->thp",
        jnp.exp(running),
        before,
        query_proj.astype(jnp.float32),
        precision=precise,
    )
    mixer_out = within + carried
    gated_out = mixer_out * jax.nn.silu(gate_input.astype(jnp.float32)).reshape(
        row_count, head_count, head_width
    )
    inv_rms = lax.rsqrt(jnp.mean(gated_out * gated_out, axis=2, keepdims=True) + 1e-05)
    normed = (gated_out * inv_rms).reshape(row_count, channels) * head_gain[None, :]
    block_out = (residual.astype(jnp.float32) + normed).astype(jnp.bfloat16)

    exp_count = lax.axis_size("exp")
    capacity = 3 * row_count // exp_count
    tables, gate_sum = route_tables(
        expert_ids, route_weight, jnp.arange(exp_count, dtype=jnp.int32), capacity
    )
    picked = jnp.einsum(
        "ekt,td->ekd",
        tables.astype(jnp.bfloat16),
        block_out,
        preferred_element_type=jnp.float32,
    ).astype(jnp.bfloat16)
    arrived = lax.all_to_all(picked, "exp", 0, 0)
    own_rows = jnp.transpose(arrived, (1, 0, 2)).reshape(capacity, exp_count * channels)
    widened = own_rows.astype(jnp.float32)
    chosen = (
        widened
        * lax.rsqrt(jnp.mean(widened * widened, axis=1, keepdims=True) + 1e-06)
        * ffn_gain[None, :]
    ).astype(jnp.bfloat16)

    gate_here = gate_weight[0]
    up_here = up_weight[0]
    down_here = down_weight[0]
    token_piece = lax.all_gather(
        lax.all_gather(chosen, "chip", axis=0, tiled=True), "core", axis=0, tiled=True
    )
    gate_proj = jnp.dot(token_piece, gate_here, preferred_element_type=jnp.float32)
    up_proj = jnp.dot(token_piece, up_here, preferred_element_type=jnp.float32)
    hidden = (jax.nn.silu(gate_proj) * up_proj).astype(jnp.bfloat16)
    partial_value = jnp.dot(hidden, down_here, preferred_element_type=jnp.float32).astype(
        jnp.bfloat16
    )
    summed = lax.psum_scatter(
        lax.psum_scatter(partial_value, "core", scatter_dimension=0, tiled=True),
        "chip",
        scatter_dimension=0,
        tiled=True,
    )
    outgoing = jnp.transpose(summed.reshape(capacity, exp_count, channels), (1, 0, 2))
    returned = lax.all_to_all(outgoing, "exp", 0, 0)
    weights = tables * gate_sum[:, None, :]
    expert_out = jnp.einsum(
        "ekt,ekd->td", weights, returned.astype(jnp.float32), precision=precise
    ).astype(jnp.bfloat16)
    return (block_out, expert_out)


def solution(mesh):
    ctx_size, exp_size = mesh.devices.shape
    split = Mesh(mesh.devices.reshape(ctx_size // 2, 2, exp_size), ("chip", "core", "exp"))
    placed = (
        P(CTX, "exp"),
        P(CTX, "exp"),
        P(CTX, None),
        P(CTX, None),
        P(CTX, "exp"),
        P("exp"),
        P("exp"),
        P(CTX, "exp"),
        P(),
        P("exp", None, CTX),
        P("exp", None, CTX),
        P("exp", CTX, None),
        P(CTX, None),
        P(CTX, None),
    )
    return jax.shard_map(
        on_device,
        mesh=split,
        in_specs=placed,
        out_specs=(P(CTX, "exp"), P(CTX, "exp")),
        check_vma=False,
    )
```

time: 406 us -> 395 us (0.973)
  other arithmetic: 40.5 us -> 7.27 us
  waiting for transfers between devices: 278 us -> 296 us
  starting transfers between devices: 0.21 us -> 7.4 us
    all_gather x3 -> x4, waiting for transfers between devices: 129 us -> 164 us  [the longest x1 62.5 us: on_device(): lax.all_gather(chosen, 'chip', axis=0, tiled=True)]
    select_n x32 -> x1, other arithmetic: 32.4 us -> 0.07 us  [carried_state(): weight = jnp.where((shard_of < me)[:, None], jnp.exp(spans), 0.0)]
    reduce_scatter x2, waiting for transfers between devices: 149 us -> 120 us  [the longest x1 91.2 us: on_device(): lax.psum_scatter(lax.psum_scatter(partial_value, 'core', scatter_dimensio...]
    all_to_all x0 -> x1, blocking collectives: none -> 21.9 us  [on_device(): arrived = lax.all_to_all(picked, 'exp', 0, 0)]
    all_gather x1 -> x0, blocking collectives: 21.7 us -> none  [carried_in(): lax.all_gather(part.astype(kind), axis)]
    all_to_all x0 -> x1, waiting for transfers between devices: none -> 12.5 us  [on_device(): returned = lax.all_to_all(outgoing, 'exp', 0, 0)]
    all_to_all x0 -> x1, starting transfers between devices: none -> 6.98 us  [on_device(): returned = lax.all_to_all(outgoing, 'exp', 0, 0)]
  transfers between devices with their start and end apart: 5 -> 7, of which waited for: 5 -> 7; matrix products, arithmetic and copies ran while one was open for 2% -> 1% of each run, Pallas kernels for 0% -> 0%
where the time goes in v1:
time: 395 us; the launch traced here: 394 us
  waiting for transfers between devices  296 us (75%)
  matrix products  39.4 us (10%)
  blocking collectives  21.9 us (6%)
  between operations  14.3 us (4%)
  local copies, waits for them, and re-layouts  7.83 us (2%)
  starting transfers between devices  7.4 us (2%)
  other arithmetic  7.27 us (2%)
    reduce_scatter x1, waiting for transfers between devices, on_device(): lax.psum_scatter(lax.psum_scatter(partial_value, 'core', scatter_dimensio...  91.2 us
    all_gather x1, waiting for transfers between devices, on_device(): lax.all_gather(chosen, 'chip', axis=0, tiled=True)  62.5 us
    all_gather x1, waiting for transfers between devices, carried_state(): by_chip = lax.all_gather(packed, 'chip')  52.8 us
    all_gather x1, waiting for transfers between devices, on_device(): lax.all_gather(lax.all_gather(chosen, 'chip', axis=0, tiled=True), 'core'...  31.2 us
    reduce_scatter x1, waiting for transfers between devices, on_device(): lax.psum_scatter(partial_value, 'core', scatter_dimension=0, tiled=True)  28.7 us
    all_to_all x1, blocking collectives, on_device(): arrived = lax.all_to_all(picked, 'exp', 0, 0)  21.9 us
    dot_general x1, matrix products, on_device(): jnp.dot(hidden, down_here, preferred_element_type=jnp.float32)  20 us
    all_gather x1, waiting for transfers between devices, carried_state(): everything = lax.all_gather(by_chip, 'core')  17.3 us
  transfers between devices with their start and end apart: 7, of which 7 were waited for; matrix products, arithmetic and copies ran while one was open for 1% of the time, Pallas kernels for 0%

profile of v1, /device:TPU:2, one launch (start us, length us, event | category | flops | bytes accessed | tf_op | source)
XLA Modules:
  0.0 394.4 jit_solution(6074835486635477294)
XLA Ops:
  7.2 0.9 negate_multiply_fusion
  8.1 0.1 copy.52
  8.3 0.2 reduce_window_sum.22
  8.5 1.0 copy.55
  9.6 1.0 convolution_convert_fusion.2
  10.6 0.2 scatter.9
  10.8 0.7 pad_maximum_fusion
  11.5 0.0 all-gather.13.cloned.1.call-start
  11.5 52.8 %all-gather.11.cloned.1.call-done = bf16[8320,128]{1,0:T(8,128)(2,1)} async-done(((bf16[520,128]{1,0:T(8,128)(2,1)}), bf16[8320,128]{1,0:T(8,128)(2,1)}) %all-gather.11.cloned.1.call-update) | async-done | bytes 2129936 | tf_op jit(solution)/shard_map/all_gather | solution.py:51
  64.4 0.1 copy.56
  64.5 1.0 convert_multiply_fusion.1
  65.5 0.8 copy.59
  66.3 0.3 reduce_window_sum.23
  66.7 0.1 compare_and_fusion
  66.7 0.9 fusion.53
  67.6 17.3 %all-gather.13.cloned.1.call-done = bf16[32,520,128]{2,1,0:T(8,128)(2,1)} async-done(((bf16[16,520,128]{2,1,0:T(8,128)(2,1)}), bf16[32,520,128]{2,1,0:T(8,128)(2,1)}) %all-gather.13.cloned.1.call-update) | async-done | bytes 4259856 | tf_op jit(solution)/shard_map/all_gather | solution.py:52
  84.9 0.9 fusion.45
  85.9 0.1 copy.58
  86.0 0.1 select_reduce_fusion
  86.1 0.1 select_bitcast_fusion
  86.2 0.1 copy.63
  86.2 2.3 slice-done
  88.5 3.5 fusion
  92.0 0.3 fusion.14
  92.3 0.8 multiply_reduce_fusion
  93.2 0.8 copy.60
  94.0 1.1 add_convert_fusion
  95.1 0.2 convolution_convert_fusion.1
  95.3 0.4 copy-done.2
  95.7 21.9 %all_to_all.10 = bf16[8,48,512]{2,1,0:T(8,128)(2,1)S(1)} all-to-all(bf16[8,48,512]{2,1,0:T(8,128)(2,1)S(1)} %convolution_convert_fusion.1), channel_id=1, replica_groups=mesh['chip'=16,'core'=2,'exp'=8] {'exp'}, dimensions={0} | all-to-all | bytes 786432 | tf_op jit(solution)/shard_map/all_to_all | solution.py:122
  117.7 0.1 convert_bitcast_fusion
  117.7 0.1 copy.67
  117.8 0.2 fusion.16
  118.0 0.9 multiply_convert_fusion
  118.9 0.0 all-gather.9.cloned.1.call-start
  119.0 62.5 %all-gather.7.cloned.1.call-done = bf16[768,4096]{1,0:T(8,128)(2,1)} async-done(((bf16[48,4096]{1,0:T(8,128)(2,1)}), bf16[768,4096]{1,0:T(8,128)(2,1)}) %all-gather.7.cloned.1.call-update) | async-done | bytes 6291472 | tf_op jit(solution)/shard_map/all_gather | solution.py:135
  181.5 0.2 reduce-scatter.3.cloned.1.call-start
  181.7 31.2 %all-gather.9.cloned.1.call-done = bf16[1536,4096]{1,0:T(8,128)(2,1)} async-done(((bf16[768,4096]{1,0:T(8,128)(2,1)}), bf16[1536,4096]{1,0:T(8,128)(2,1)}) %all-gather.9.cloned.1.call-update) | async-done | bytes 12582928 | tf_op jit(solution)/shard_map/all_gather | solution.py:134
  213.0 11.6 %fusion.4 = f32[1536,384]{1,0:T(8,128)} fusion(bf16[1536,4096]{1,0:T(8,128)(2,1)} %all-gather.9.cloned.1.call-done, bf16[1,4096,384]{2,1,0:T(8,128)(2,1)} %param.27), kind=kOutput, calls=%fused_computation.6 | convolution fusion | flops 4831838208 | bytes 18087936 | tf_op jit(solution)/shard_map/dot_general | solution.py:137
  224.5 20.0 %convolution_convert_fusion = bf16[1536,4096]{1,0:T(8,128)(2,1)} fusion(bf16[1,384,4096]{2,1,0:T(8,128)(2,1)S(1)} %copy-done, bf16[1536,4096]{1,0:T(8,128)(2,1)} %all-gather.9.cloned.1.call-done, bf16[1,4096,384]{2,1,0:T(8,128)(2,1)} %param.28, f32[1536,384]{1,0:T(8,128)} %fusion.4), kind=kOutput, calls=%fused_computation | convolution fusion | flops 9673506816 | bytes 33816576 | tf_op jit(solution)/shard_map/dot_general | solution.py:140
  244.6 0.0 reduce-scatter.5.cloned.1.call-start
  244.6 28.7 %reduce-scatter.3.cloned.1.call-done = bf16[768,4096]{1,0:T(8,128)(2,1)} async-done(((bf16[1536,4096]{1,0:T(8,128)(2,1)}), bf16[768,4096]{1,0:T(8,128)(2,1)}) %reduce-scatter.3.cloned.1.call-update) | async-done | bytes 6291472 | tf_op jit(solution)/shard_map/reduce_scatter | solution.py:144
  273.3 91.2 %reduce-scatter.5.cloned.1.call-done = bf16[48,4096]{1,0:T(8,128)(2,1)} async-done(((bf16[768,4096]{1,0:T(8,128)(2,1)}), bf16[48,4096]{1,0:T(8,128)(2,1)}) %reduce-scatter.5.cloned.1.call-update) | async-done | bytes 393232 | tf_op jit(solution)/shard_map/reduce_scatter | solution.py:143
  364.5 1.8 copy.71
  366.3 7.0 %all-to-all-start.1 = ((bf16[8,48,512]{2,1,0:T(8,128)(2,1)}), bf16[8,48,512]{2,1,0:T(8,128)(2,1)S(1)}, u32[]{:S(2)}, u32[]{:S(2)}) async-start(bf16[8,48,512]{2,1,0:T(8,128)(2,1)} %bitcast.71), calls=%async_computation.3 | async-start | bytes 786432 | tf_op jit(solution)/shard_map/all_to_all | solution.py:150
  373.3 0.7 select_reduce_fusion.1
  374.0 12.5 %all-to-all-done.1 = bf16[8,48,512]{2,1,0:T(8,128)(2,1)S(1)} async-done(((bf16[8,48,512]{2,1,0:T(8,128)(2,1)}), bf16[8,48,512]{2,1,0:T(8,128)(2,1)S(1)}, u32[]{:S(2)}, u32[]{:S(2)}) %all-to-all-start.1) | async-done | bytes 393248 | tf_op jit(solution)/shard_map/all_to_all | solution.py:150
  386.5 1.1 fusion.15
  (39 shorter events, 0.4 us)
Async XLA Ops:
  7.2 217.4 %copy-start = (bf16[1,384,4096]{2,1,0:T(8,128)(2,1)S(1)}, bf16[1,384,4096]{2,1,0:T(8,128)(2,1)}, u32[]{:S(2)}) copy-start(bf16[1,384,4096]{2,1,0:T(8,128)(2,1)} %param.29) | copy-start | bytes 9437188
  7.2 59.1 %copy-start.6 = (s32[128,2]{0,1:T(2,128)S(1)}, s32[128,2]{0,1:T(2,128)}, u32[]{:S(2)}) copy-start(s32[128,2]{0,1:T(2,128)} %param.30) | copy-start | bytes 3076
  7.2 57.1 %all-gather.11.cloned.1.call-start = ((), (), s32[]{:S(2)}) async-start(), calls=%async_computation.8 | async-start | bytes 2263040 | tf_op jit(solution)/shard_map/all_gather | solution.py:51
  11.5 73.5 %all-gather.13.cloned.1.call-start = ((), (), s32[]{:S(2)}) async-start(), calls=%async_computation.9 | async-start | bytes 6389760 | tf_op jit(solution)/shard_map/all_gather | solution.py:52
  64.3 117.2 %all-gather.7.cloned.1.call-start = ((), (), s32[]{:S(2)}) async-start(), calls=%async_computation.4 | async-start | bytes 6684672 | tf_op jit(solution)/shard_map/all_gather | solution.py:135
  86.2 2.3 slice-start
  86.2 5.8 %copy-start.4 = (bf16[128,128]{1,0:T(8,128)(2,1)S(1)}, bf16[128,128]{1,0:T(8,128)(2,1)}, u32[]{:S(2)}) copy-start(bf16[128,128]{1,0:T(8,128)(2,1)} %param.21) | copy-start | bytes 98308
  86.2 6.1 %copy-start.3 = (f32[128,512]{0,1:T(8,128)S(1)}, f32[128,512]{0,1:T(8,128)}, u32[]{:S(2)}) copy-start(f32[128,512]{0,1:T(8,128)} %copy.59) | copy-start | bytes 786436
  93.1 24.9 %copy-start.5 = (f32[4096]{0:T(1024)S(1)}, f32[4096]{0:T(1024)}, u32[]{:S(2)}) copy-start(f32[4096]{0:T(1024)} %param.26) | copy-start | bytes 49156
  95.1 0.7 copy-start.2
  118.9 94.0 %all-gather.9.cloned.1.call-start = ((), (), s32[]{:S(2)}) async-start(), calls=%async_computation.5 | async-start | bytes 18874368 | tf_op jit(solution)/shard_map/all_gather | solution.py:134
  181.5 91.8 %reduce-scatter.3.cloned.1.call-start = ((), (), s32[]{:S(2)}) async-start(), calls=%async_computation.6 | async-start | bytes 18874368 | tf_op jit(solution)/shard_map/reduce_scatter | solution.py:144
  244.6 120.0 %reduce-scatter.5.cloned.1.call-start = ((), (), s32[]{:S(2)}) async-start(), calls=%async_computation.7 | async-start | bytes 6684672 | tf_op jit(solution)/shard_map/reduce_scatter | solution.py:143
  273.3 114.2 %copy-start.1 = (bf16[1,384,4096]{2,1,0:T(8,128)(2,1)S(1)}, bf16[1,384,4096]{2,1,0:T(8,128)(2,1)}, u32[]{:S(2)}) copy-start(bf16[1,384,4096]{2,1,0:T(8,128)(2,1)} %param.29) | copy-start | bytes 9437188
  273.3 100.0 %copy-start.7 = (s32[128,2]{0,1:T(2,128)S(1)}, s32[128,2]{0,1:T(2,128)}, u32[]{:S(2)}) copy-start(s32[128,2]{0,1:T(2,128)} %param.30) | copy-start | bytes 3076
  366.3 20.1 %all-to-all-start.1 = ((bf16[8,48,512]{2,1,0:T(8,128)(2,1)}), bf16[8,48,512]{2,1,0:T(8,128)(2,1)S(1)}, u32[]{:S(2)}, u32[]{:S(2)}) async-start(bf16[8,48,512]{2,1,0:T(8,128)(2,1)} %bitcast.71), calls=%async_computation.3 | async-start | bytes 786432 | tf_op jit(solution)/shard_map/all_to_all | solution.py:150
Sparse Core Ops, SparseCore 0:
  11.6 52.6 all-gather.10
  66.1 18.8 all-gather.12
  119.1 62.3 all-gather.6
  183.2 29.7 all-gather.8
  244.7 28.5 reduce-scatter.2
  276.9 87.5 reduce-scatter.4

commit v2 on v1

--- a/solution.py
+++ b/solution.py
@@ -1,10 +1,9 @@
 import jax
 import jax.numpy as jnp
 from jax import lax
-from jax.sharding import Mesh, PartitionSpec as P
+from jax.sharding import PartitionSpec as P
 
 precise = lax.Precision.HIGHEST
-CTX = ("chip", "core")
 
 
 def local_block(ssm_piece, key_piece, query_piece, step_piece, decay_rate, head_count):
@@ -40,34 +39,29 @@
 
 def carried_state(overall, states):
     head_count, head_width, nstate = states.shape
-    flat = states.astype(jnp.bfloat16).reshape(head_count * head_width, nstate)
-    high = overall.astype(jnp.bfloat16)
-    low = (overall - high.astype(jnp.float32)).astype(jnp.bfloat16)
-    extra = jnp.zeros((8, nstate), jnp.bfloat16)
-    extra = extra.at[0, :head_count].set(high).at[1, :head_count].set(low)
-    packed = jnp.concatenate([flat, extra], axis=0)
-    chips = lax.axis_size("chip")
-    cores = lax.axis_size("core")
-    by_chip = lax.all_gather(packed, "chip")
-    everything = lax.all_gather(by_chip, "core")
-    shards = chips * cores
-    everything = everything.reshape(shards, packed.shape[0], nstate)
-    core_of = jnp.arange(shards, dtype=jnp.int32) // chips
-    chip_of = jnp.arange(shards, dtype=jnp.int32) % chips
-    shard_of = chip_of * cores + core_of
-    me = lax.axis_index("chip") * cores + lax.axis_index("core")
+    shards = lax.axis_size("ctx")
     rows = head_count * head_width
-    decay_all = (
-        everything[:, rows, :head_count].astype(jnp.float32)
-        + everything[:, rows + 1, :head_count].astype(jnp.float32)
-    )
-    between = (shard_of[:, None] < shard_of[None, :]) & (shard_of[None, :] < me)
-    spans = jnp.sum(jnp.where(between[:, :, None], decay_all[None, :, :], 0.0), axis=1)
-    weight = jnp.where((shard_of < me)[:, None], jnp.exp(spans), 0.0)
-    gathered = everything[:, :rows, :].astype(jnp.float32).reshape(
-        shards, head_count, head_width, nstate
-    )
-    return jnp.einsum("kh,khpn->hpn", weight, gathered, precision=precise)
+    extra = jnp.zeros((8, nstate), jnp.float32).at[0, :head_count].set(overall)
+    packed = jnp.concatenate([states.reshape(rows, nstate), extra], axis=0)
+
+    def shift(value, distance):
+        pairs = [(i, i + distance) for i in range(shards - distance)]
+        return lax.ppermute(value, "ctx", pairs)
+
+    packed = shift(packed, 1)
+    distance = 1
+    while distance < shards:
+        earlier = shift(packed, distance)
+        decay = packed[rows, :head_count]
+        joined = (
+            jnp.exp(decay)[:, None, None] * earlier[:rows].reshape(head_count, head_width, nstate)
+            + packed[:rows].reshape(head_count, head_width, nstate)
+        )
+        packed = jnp.concatenate(
+            [joined.reshape(rows, nstate), earlier[rows:] + packed[rows:]], axis=0
+        )
+        distance *= 2
+    return packed[:rows].reshape(head_count, head_width, nstate)
 
 
 def on_device(
@@ -131,21 +125,14 @@
     gate_here = gate_weight[0]
     up_here = up_weight[0]
     down_here = down_weight[0]
-    token_piece = lax.all_gather(
-        lax.all_gather(chosen, "chip", axis=0, tiled=True), "core", axis=0, tiled=True
-    )
+    token_piece = lax.all_gather(chosen, "ctx", axis=0, tiled=True)
     gate_proj = jnp.dot(token_piece, gate_here, preferred_element_type=jnp.float32)
     up_proj = jnp.dot(token_piece, up_here, preferred_element_type=jnp.float32)
     hidden = (jax.nn.silu(gate_proj) * up_proj).astype(jnp.bfloat16)
     partial_value = jnp.dot(hidden, down_here, preferred_element_type=jnp.float32).astype(
         jnp.bfloat16
     )
-    summed = lax.psum_scatter(
-        lax.psum_scatter(partial_value, "core", scatter_dimension=0, tiled=True),
-        "chip",
-        scatter_dimension=0,
-        tiled=True,
-    )
+    summed = lax.psum_scatter(partial_value, "ctx", scatter_dimension=0, tiled=True)
     outgoing = jnp.transpose(summed.reshape(capacity, exp_count, channels), (1, 0, 2))
     returned = lax.all_to_all(outgoing, "exp", 0, 0)
     weights = tables * gate_sum[:, None, :]
@@ -156,28 +143,26 @@
 
 
 def solution(mesh):
-    ctx_size, exp_size = mesh.devices.shape
-    split = Mesh(mesh.devices.reshape(ctx_size // 2, 2, exp_size), ("chip", "core", "exp"))
     placed = (
-        P(CTX, "exp"),
-        P(CTX, "exp"),
-        P(CTX, None),
-        P(CTX, None),
-        P(CTX, "exp"),
+        P("ctx", "exp"),
+        P("ctx", "exp"),
+        P("ctx", None),
+        P("ctx", None),
+        P("ctx", "exp"),
         P("exp"),
         P("exp"),
-        P(CTX, "exp"),
+        P("ctx", "exp"),
         P(),
-        P("exp", None, CTX),
-        P("exp", None, CTX),
-        P("exp", CTX, None),
-        P(CTX, None),
-        P(CTX, None),
+        P("exp", None, "ctx"),
+        P("exp", None, "ctx"),
+        P("exp", "ctx", None),
+        P("ctx", None),
+        P("ctx", None),
     )
     return jax.shard_map(
         on_device,
-        mesh=split,
+        mesh=mesh,
         in_specs=placed,
-        out_specs=(P(CTX, "exp"), P(CTX, "exp")),
+        out_specs=(P("ctx", "exp"), P("ctx", "exp")),
         check_vma=False,
     )

time: 395 us -> 350 us (0.89)
  waiting for transfers between devices: 296 us -> 210 us
  starting transfers between devices: 7.4 us -> 33.4 us
  other arithmetic: 7.27 us -> 20.7 us
  local copies, waits for them, and re-layouts: 7.83 us -> 11.9 us
    all_gather x4 -> x1, waiting for transfers between devices: 164 us -> 67.2 us  [on_device(): token_piece = lax.all_gather(chosen, 'ctx', axis=0, tiled=True)]
    ppermute x0 -> x6, starting transfers between devices: none -> 26.3 us  [shift(): return lax.ppermute(value, 'ctx', pairs)]
    ppermute x0 -> x6, waiting for transfers between devices: none -> 18.8 us  [shift(): return lax.ppermute(value, 'ctx', pairs)]
    add x2 -> x8, other arithmetic: 0.95 us -> 9.84 us  [the longest x4 7.11 us: carried_state(): jnp.exp(decay)[:, None, None]]
    reduce_scatter x2 -> x1, waiting for transfers between devices: 120 us -> 111 us  [on_device(): lax.psum_scatter(partial_value, 'ctx', scatter_dimension=0, tiled=True)]
  transfers between devices with their start and end apart: 7 -> 9, of which waited for: 7 -> 9; matrix products, arithmetic and copies ran while one was open for 1% -> 3% of each run, Pallas kernels for 0% -> 0%
where the time goes in v2:
time: 350 us; the launch traced here: 349 us
  waiting for transfers between devices  210 us (60%)
  matrix products  38.8 us (11%)
  starting transfers between devices  33.4 us (10%)
  other arithmetic  20.7 us (6%)
  blocking collectives  20.1 us (6%)
  between operations  14.3 us (4%)
  local copies, waits for them, and re-layouts  11.9 us (3%)
    reduce_scatter x1, waiting for transfers between devices, on_device(): lax.psum_scatter(partial_value, 'ctx', scatter_dimension=0, tiled=True)  111 us
    all_gather x1, waiting for transfers between devices, on_device(): token_piece = lax.all_gather(chosen, 'ctx', axis=0, tiled=True)  67.2 us
    ppermute x6, starting transfers between devices, shift(): return lax.ppermute(value, 'ctx', pairs)  26.3 us
    all_to_all x1, blocking collectives, on_device(): arrived = lax.all_to_all(picked, 'exp', 0, 0)  20.1 us
    dot_general x1, matrix products, on_device(): jnp.dot(hidden, down_here, preferred_element_type=jnp.float32)  20 us
    ppermute x6, waiting for transfers between devices, shift(): return lax.ppermute(value, 'ctx', pairs)  18.8 us
    all_to_all x1, waiting for transfers between devices, on_device(): returned = lax.all_to_all(outgoing, 'exp', 0, 0)  12.4 us
    dot_general x1, matrix products, on_device(): jnp.dot(token_piece, gate_here, preferred_element_type=jnp.float32)  11.6 us
  transfers between devices with their start and end apart: 9, of which 9 were waited for; matrix products, arithmetic and copies ran while one was open for 3% of the time, Pallas kernels for 0%

profile of v2, /device:TPU:2, one launch (start us, length us, event | category | flops | bytes accessed | tf_op | source)
XLA Modules:
  0.0 348.9 jit_solution(7775336017658809662)
XLA Ops:
  7.2 0.9 negate_multiply_fusion
  8.5 1.0 copy.43
  9.6 1.0 fusion.33
  10.7 1.9 collective-permute-start
  12.6 1.7 convert_multiply_fusion.1
  14.3 4.2 %collective-permute-done = f32[520,128]{1,0:T(8,128)} collective-permute-done((f32[520,128]{1,0:T(8,128)S(1)}, f32[520,128]{1,0:T(8,128)}, u32[]{:S(2)}, u32[]{:S(2)}) %collective-permute-start) | collective-permute-done | bytes 266272 | tf_op jit(solution)/shard_map/ppermute | solution.py:49
  18.5 1.9 collective-permute-start.1
  20.4 1.6 fusion.65
  22.0 0.7 fusion.60
  23.4 3.1 collective-permute-done.1
  26.5 0.7 slice_add_fusion.3
  27.2 1.9 multiply_add_fusion.3
  29.1 0.7 pad_maximum_fusion
  29.8 3.4 collective-permute-start.2
  34.5 5.0 %collective-permute-done.2 = f32[520,128]{1,0:T(8,128)} collective-permute-done((f32[520,128]{1,0:T(8,128)}, f32[520,128]{1,0:T(8,128)}, u32[]{:S(2)}, u32[]{:S(2)}) %collective-permute-start.2) | collective-permute-done | bytes 266272 | tf_op jit(solution)/shard_map/ppermute | solution.py:49
  39.5 0.7 slice_add_fusion.2
  40.1 1.7 multiply_add_fusion.2
  41.8 0.7 copy-done.1
  42.6 0.7 pad_maximum_fusion.1
  43.3 7.0 %collective-permute-start.3 = (f32[520,128]{1,0:T(8,128)}, f32[520,128]{1,0:T(8,128)}, u32[]{:S(2)}, u32[]{:S(2)}) collective-permute-start(f32[520,128]{1,0:T(8,128)} %pad_maximum_fusion.1), channel_id=1, source_target_pairs={{0,32},{8,40},{16,48},{24,56},{32,64},{40,72},{48,80},{56,88},{64,... | collective-permute-start | bytes 798728 | tf_op jit(solution)/shard_map/ppermute | solution.py:49
  50.2 0.7 broadcast_compare_fusion
  52.0 3.1 collective-permute-done.3
  55.1 0.7 slice_add_fusion.1
  55.8 1.8 multiply_add_fusion.1
  57.6 0.7 pad_maximum_fusion.2
  58.3 5.1 %collective-permute-start.4 = (f32[520,128]{1,0:T(8,128)}, f32[520,128]{1,0:T(8,128)}, u32[]{:S(2)}, u32[]{:S(2)}) collective-permute-start(f32[520,128]{1,0:T(8,128)} %pad_maximum_fusion.2), channel_id=1, source_target_pairs={{0,64},{8,72},{16,80},{24,88},{32,96},{40,104},{48,112},{56,120},{... | collective-permute-start | bytes 798728 | tf_op jit(solution)/shard_map/ppermute | solution.py:49
  64.7 2.3 collective-permute-done.4
  67.6 1.7 multiply_add_fusion
  69.4 0.7 pad_maximum_fusion.3
  70.1 7.0 %collective-permute-start.5 = (f32[520,128]{1,0:T(8,128)}, f32[520,128]{1,0:T(8,128)}, u32[]{:S(2)}, u32[]{:S(2)}) collective-permute-start(f32[520,128]{1,0:T(8,128)} %pad_maximum_fusion.3), channel_id=1, source_target_pairs={{0,128},{8,136},{16,144},{24,152},{32,160},{40,168},{48,176},{56,1... | collective-permute-start | bytes 798728 | tf_op jit(solution)/shard_map/ppermute | solution.py:49
  78.4 1.1 copy.46
  79.5 1.1 collective-permute-done.5
  80.6 1.0 slice.96
  81.6 1.7 fusion.12
  83.3 1.6 multiply_reduce_fusion
  85.0 0.8 copy.47
  85.8 1.1 add_convert_fusion
  87.5 20.1 %all_to_all.10 = bf16[8,48,512]{2,1,0:T(8,128)(2,1)S(1)} all-to-all(bf16[8,48,512]{2,1,0:T(8,128)(2,1)S(1)} %convolution_convert_fusion.1), channel_id=1, replica_groups=mesh['ctx'=32,'exp'=8] {'exp'}, dimensions={0} | all-to-all | bytes 786432 | tf_op jit(solution)/shard_map/all_to_all | solution.py:116
  108.0 0.9 multiply_convert_fusion
  109.0 67.2 %all-gather.2.cloned.1.call-done = bf16[1536,4096]{1,0:T(8,128)(2,1)} async-done(((bf16[48,4096]{1,0:T(8,128)(2,1)}), bf16[1536,4096]{1,0:T(8,128)(2,1)}) %all-gather.2.cloned.1.call-update) | async-done | bytes 12582928 | tf_op jit(solution)/shard_map/all_gather | solution.py:128
  176.2 11.6 %fusion.2 = f32[1536,384]{1,0:T(8,128)} fusion(bf16[1536,4096]{1,0:T(8,128)(2,1)} %all-gather.2.cloned.1.call-done, bf16[1,4096,384]{2,1,0:T(8,128)(2,1)} %param.25), kind=kOutput, calls=%fused_computation.4 | convolution fusion | flops 4831838208 | bytes 18087936 | tf_op jit(solution)/shard_map/dot_general | solution.py:129
  187.8 20.0 %convolution_convert_fusion = bf16[1536,4096]{1,0:T(8,128)(2,1)} fusion(bf16[1,384,4096]{2,1,0:T(8,128)(2,1)S(1)} %copy-done, bf16[1536,4096]{1,0:T(8,128)(2,1)} %all-gather.2.cloned.1.call-done, bf16[1,4096,384]{2,1,0:T(8,128)(2,1)} %param.26, f32[1536,384]{1,0:T(8,128)} %fusion.2), kind=kOutput, calls=%fused_computation | convolution fusion | flops 9673506816 | bytes 33816576 | tf_op jit(solution)/shard_map/dot_general | solution.py:132
  207.8 111.2 %reduce-scatter.2.cloned.1.call-done = bf16[48,4096]{1,0:T(8,128)(2,1)} async-done(((bf16[1536,4096]{1,0:T(8,128)(2,1)}), bf16[48,4096]{1,0:T(8,128)(2,1)}) %reduce-scatter.2.cloned.1.call-update) | async-done | bytes 393232 | tf_op jit(solution)/shard_map/reduce_scatter | solution.py:135
  319.0 1.8 copy.53
  320.8 7.0 %all-to-all-start.1 = ((bf16[8,48,512]{2,1,0:T(8,128)(2,1)}), bf16[8,48,512]{2,1,0:T(8,128)(2,1)S(1)}, u32[]{:S(2)}, u32[]{:S(2)}) async-start(bf16[8,48,512]{2,1,0:T(8,128)(2,1)} %bitcast.76), calls=%async_computation.2 | async-start | bytes 786432 | tf_op jit(solution)/shard_map/all_to_all | solution.py:137
  327.8 0.7 select_reduce_fusion
  328.5 12.4 %all-to-all-done.1 = bf16[8,48,512]{2,1,0:T(8,128)(2,1)S(1)} async-done(((bf16[8,48,512]{2,1,0:T(8,128)(2,1)}), bf16[8,48,512]{2,1,0:T(8,128)(2,1)S(1)}, u32[]{:S(2)}, u32[]{:S(2)}) %all-to-all-start.1) | async-done | bytes 393248 | tf_op jit(solution)/shard_map/all_to_all | solution.py:137
  340.9 1.1 fusion.13
  (59 shorter events, 7.8 us)
Async XLA Ops:
  7.2 180.6 %copy-start = (bf16[1,384,4096]{2,1,0:T(8,128)(2,1)S(1)}, bf16[1,384,4096]{2,1,0:T(8,128)(2,1)}, u32[]{:S(2)}) copy-start(bf16[1,384,4096]{2,1,0:T(8,128)(2,1)} %param.27) | copy-start | bytes 9437188
  7.2 26.0 %copy-start.6 = (s32[128,2]{0,1:T(2,128)S(1)}, s32[128,2]{0,1:T(2,128)}, u32[]{:S(2)}) copy-start(s32[128,2]{0,1:T(2,128)} %param.28) | copy-start | bytes 3076
  7.2 169.0 %all-gather.2.cloned.1.call-start = ((), (), s32[]{:S(2)}) async-start(), calls=%async_computation.3 | async-start | bytes 12976128 | tf_op jit(solution)/shard_map/all_gather | solution.py:128
  9.6 17.0 %copy-start.2 = (bf16[128,512]{0,1:T(8,128)(2,1)}, bf16[128,512]{0,1:T(8,128)(2,1)S(1)}, u32[]{:S(2)}) copy-start(bf16[128,512]{0,1:T(8,128)(2,1)S(1)} %copy.43) | copy-start | bytes 393220
  10.7 7.8 %collective-permute-start = (f32[520,128]{1,0:T(8,128)S(1)}, f32[520,128]{1,0:T(8,128)}, u32[]{:S(2)}, u32[]{:S(2)}) collective-permute-start(f32[520,128]{1,0:T(8,128)S(1)} %select_maximum_fusion), channel_id=1, source_target_pairs={{0,8},{8,16},{16,24},{24,32},{32,40},{40,48},{48,56},{56,64},{64,7... | collective-permute-start | bytes 798728 | tf_op jit(solution)/shard_map/ppermute | solution.py:49
  18.5 8.0 %collective-permute-start.1 = (f32[520,128]{1,0:T(8,128)}, f32[520,128]{1,0:T(8,128)}, u32[]{:S(2)}, u32[]{:S(2)}) collective-permute-start(f32[520,128]{1,0:T(8,128)} %collective-permute-done), channel_id=1, source_target_pairs={{0,8},{8,16},{16,24},{24,32},{32,40},{40,48},{48,56},{56,64},{64,7... | collective-permute-start | bytes 798728 | tf_op jit(solution)/shard_map/ppermute | solution.py:49
  22.7 0.6 copy-start.8
  29.8 9.6 %collective-permute-start.2 = (f32[520,128]{1,0:T(8,128)}, f32[520,128]{1,0:T(8,128)}, u32[]{:S(2)}, u32[]{:S(2)}) collective-permute-start(f32[520,128]{1,0:T(8,128)} %pad_maximum_fusion), channel_id=1, source_target_pairs={{0,16},{8,24},{16,32},{24,40},{32,48},{40,56},{48,64},{56,72},{64,... | collective-permute-start | bytes 798728 | tf_op jit(solution)/shard_map/ppermute | solution.py:49
  33.8 0.5 copy-start.9
  41.8 0.7 copy-start.1
  43.3 11.8 %collective-permute-start.3 = (f32[520,128]{1,0:T(8,128)}, f32[520,128]{1,0:T(8,128)}, u32[]{:S(2)}, u32[]{:S(2)}) collective-permute-start(f32[520,128]{1,0:T(8,128)} %pad_maximum_fusion.1), channel_id=1, source_target_pairs={{0,32},{8,40},{16,48},{24,56},{32,64},{40,72},{48,80},{56,88},{64,... | collective-permute-start | bytes 798728 | tf_op jit(solution)/shard_map/ppermute | solution.py:49
  51.2 0.8 copy-start.10
  58.3 8.6 %collective-permute-start.4 = (f32[520,128]{1,0:T(8,128)}, f32[520,128]{1,0:T(8,128)}, u32[]{:S(2)}, u32[]{:S(2)}) collective-permute-start(f32[520,128]{1,0:T(8,128)} %pad_maximum_fusion.2), channel_id=1, source_target_pairs={{0,64},{8,72},{16,80},{24,88},{32,96},{40,104},{48,112},{56,120},{... | collective-permute-start | bytes 798728 | tf_op jit(solution)/shard_map/ppermute | solution.py:49
  63.4 0.5 copy-start.11
  69.4 13.9 %copy-start.3 = (bf16[128,512]{0,1:T(8,128)(2,1)S(1)}, bf16[128,512]{0,1:T(8,128)(2,1)}, u32[]{:S(2)}) copy-start(bf16[128,512]{0,1:T(8,128)(2,1)} %copy-done.2) | copy-start | bytes 393220
  70.1 10.5 %collective-permute-start.5 = (f32[520,128]{1,0:T(8,128)}, f32[520,128]{1,0:T(8,128)}, u32[]{:S(2)}, u32[]{:S(2)}) collective-permute-start(f32[520,128]{1,0:T(8,128)} %pad_maximum_fusion.3), channel_id=1, source_target_pairs={{0,128},{8,136},{16,144},{24,152},{32,160},{40,168},{48,176},{56,1... | collective-permute-start | bytes 798728 | tf_op jit(solution)/shard_map/ppermute | solution.py:49
  84.9 23.1 %copy-start.5 = (f32[4096]{0:T(1024)S(1)}, f32[4096]{0:T(1024)}, u32[]{:S(2)}) copy-start(f32[4096]{0:T(1024)} %param.24) | copy-start | bytes 49156
  86.9 0.7 copy-start.4
  109.0 210.0 %reduce-scatter.2.cloned.1.call-start = ((), (), s32[]{:S(2)}) async-start(), calls=%async_computation.4 | async-start | bytes 12976128 | tf_op jit(solution)/shard_map/reduce_scatter | solution.py:135
  207.8 120.0 %copy-start.7 = (s32[128,2]{0,1:T(2,128)S(1)}, s32[128,2]{0,1:T(2,128)}, u32[]{:S(2)}) copy-start(s32[128,2]{0,1:T(2,128)} %param.28) | copy-start | bytes 3076
  320.8 20.1 %all-to-all-start.1 = ((bf16[8,48,512]{2,1,0:T(8,128)(2,1)}), bf16[8,48,512]{2,1,0:T(8,128)(2,1)S(1)}, u32[]{:S(2)}, u32[]{:S(2)}) async-start(bf16[8,48,512]{2,1,0:T(8,128)(2,1)} %bitcast.76), calls=%async_computation.2 | async-start | bytes 786432 | tf_op jit(solution)/shard_map/all_to_all | solution.py:137
Sparse Core Ops, SparseCore 0:
  109.1 67.0 all-gather.1
  207.9 111.0 reduce-scatter.1

commit v3 on v2

--- a/solution.py
+++ b/solution.py
@@ -39,29 +39,27 @@
 
 def carried_state(overall, states):
     head_count, head_width, nstate = states.shape
-    shards = lax.axis_size("ctx")
     rows = head_count * head_width
-    extra = jnp.zeros((8, nstate), jnp.float32).at[0, :head_count].set(overall)
-    packed = jnp.concatenate([states.reshape(rows, nstate), extra], axis=0)
-
-    def shift(value, distance):
-        pairs = [(i, i + distance) for i in range(shards - distance)]
-        return lax.ppermute(value, "ctx", pairs)
-
-    packed = shift(packed, 1)
-    distance = 1
-    while distance < shards:
-        earlier = shift(packed, distance)
-        decay = packed[rows, :head_count]
-        joined = (
-            jnp.exp(decay)[:, None, None] * earlier[:rows].reshape(head_count, head_width, nstate)
-            + packed[:rows].reshape(head_count, head_width, nstate)
-        )
-        packed = jnp.concatenate(
-            [joined.reshape(rows, nstate), earlier[rows:] + packed[rows:]], axis=0
-        )
-        distance *= 2
-    return packed[:rows].reshape(head_count, head_width, nstate)
+    high = overall.astype(jnp.bfloat16)
+    low = (overall - high.astype(jnp.float32)).astype(jnp.bfloat16)
+    extra = jnp.zeros((8, nstate), jnp.bfloat16)
+    extra = extra.at[0, :head_count].set(high).at[1, :head_count].set(low)
+    packed = jnp.concatenate([states.astype(jnp.bfloat16).reshape(rows, nstate), extra], axis=0)
+    everything = lax.all_gather(packed, "ctx")
+    shards = everything.shape[0]
+    me = lax.axis_index("ctx")
+    decay_all = (
+        everything[:, rows, :head_count].astype(jnp.float32)
+        + everything[:, rows + 1, :head_count].astype(jnp.float32)
+    )
+    shard_of = jnp.arange(shards, dtype=jnp.int32)
+    between = (shard_of[:, None] < shard_of[None, :]) & (shard_of[None, :] < me)
+    spans = jnp.sum(jnp.where(between[:, :, None], decay_all[None, :, :], 0.0), axis=1)
+    weight = jnp.where((shard_of < me)[:, None], jnp.exp(spans), 0.0)
+    gathered = everything[:, :rows, :].astype(jnp.float32).reshape(
+        shards, head_count, head_width, nstate
+    )
+    return jnp.sum(weight[:, :, None, None] * gathered, axis=0)
 
 
 def on_device(

time: 350 us -> 334 us (0.954)
  starting transfers between devices: 33.4 us -> 7.14 us
  waiting for transfers between devices: 210 us -> 235 us
  other arithmetic: 20.7 us -> 11.4 us
  local copies, waits for them, and re-layouts: 11.9 us -> 6.7 us
    all_gather x0 -> x1, waiting for transfers between devices: none -> 49.3 us  [carried_state(): everything = lax.all_gather(packed, 'ctx')]
    ppermute x6 -> x0, starting transfers between devices: 26.3 us -> none  [shift(): return lax.ppermute(value, 'ctx', pairs)]
    ppermute x6 -> x0, waiting for transfers between devices: 18.8 us -> none  [shift(): return lax.ppermute(value, 'ctx', pairs)]
    add x8 -> x1, other arithmetic: 9.84 us -> 0.01 us  [carried_state(): everything[:, rows, :head_count].astype(jnp.float32)]
    all_gather x1, waiting for transfers between devices: 67.2 us -> 62.5 us  [on_device(): token_piece = lax.all_gather(chosen, 'ctx', axis=0, tiled=True)]
    reduce_sum x0 -> x2, other arithmetic: none -> 4.58 us  [the longest x1 4.46 us: carried_state(): return jnp.sum(weight[:, :, None, None] * gathered, axis=0)]
  transfers between devices with their start and end apart: 9 -> 4, of which waited for: 9 -> 4; matrix products, arithmetic and copies ran while one was open for 3% -> 2% of each run, Pallas kernels for 0% -> 0%
where the time goes in v3:
time: 334 us; the launch traced here: 333 us
  waiting for transfers between devices  235 us (70%)
  matrix products  36.5 us (11%)
  blocking collectives  21.9 us (7%)
  between operations  14 us (4%)
  other arithmetic  11.4 us (3%)
  starting transfers between devices  7.14 us (2%)
  local copies, waits for them, and re-layouts  6.7 us (2%)
    reduce_scatter x1, waiting for transfers between devices, on_device(): lax.psum_scatter(partial_value, 'ctx', scatter_dimension=0, tiled=True)  111 us
    all_gather x1, waiting for transfers between devices, on_device(): token_piece = lax.all_gather(chosen, 'ctx', axis=0, tiled=True)  62.5 us
    all_gather x1, waiting for transfers between devices, carried_state(): everything = lax.all_gather(packed, 'ctx')  49.3 us
    all_to_all x1, blocking collectives, on_device(): arrived = lax.all_to_all(picked, 'exp', 0, 0)  21.9 us
    dot_general x1, matrix products, on_device(): jnp.dot(hidden, down_here, preferred_element_type=jnp.float32)  20 us
    all_to_all x1, waiting for transfers between devices, on_device(): returned = lax.all_to_all(outgoing, 'exp', 0, 0)  12.4 us
    dot_general x1, matrix products, on_device(): jnp.dot(token_piece, gate_here, preferred_element_type=jnp.float32)  11.5 us
    all_to_all x1, starting transfers between devices, on_device(): returned = lax.all_to_all(outgoing, 'exp', 0, 0)  7.01 us
  transfers between devices with their start and end apart: 4, of which 4 were waited for; matrix products, arithmetic and copies ran while one was open for 2% of the time, Pallas kernels for 0%

profile of v3, /device:TPU:2, one launch (start us, length us, event | category | flops | bytes accessed | tf_op | source)
XLA Modules:
  0.0 333.1 jit_solution(7148985578845104388)
XLA Ops:
  7.2 0.0 all-gather.6.cloned.1.call-start
  7.2 0.9 negate_multiply_fusion
  8.1 0.1 copy.40
  8.2 0.2 reduce_window_sum.22
  8.5 1.0 copy.43
  9.6 1.0 convolution_convert_fusion.2
  10.6 0.2 scatter.9
  10.8 0.7 pad_maximum_fusion
  11.4 0.0 all-gather.6.cloned.1.call-update
  11.5 0.0 all-gather.4.cloned.1.call-start
  11.6 0.1 copy.44
  11.6 1.0 convert_multiply_fusion.1
  12.6 0.8 copy.48
  13.5 0.7 fusion.44
  14.2 0.3 reduce_window_sum.23
  14.5 1.6 fusion.50
  16.1 49.3 %all-gather.6.cloned.1.call-done = bf16[16640,128]{1,0:T(8,128)(2,1)} async-done(((bf16[520,128]{1,0:T(8,128)(2,1)}), bf16[16640,128]{1,0:T(8,128)(2,1)}) %all-gather.6.cloned.1.call-update) | async-done | bytes 4259856 | tf_op jit(solution)/shard_map/all_gather | solution.py:48
  65.3 0.9 fusion.48
  66.3 0.1 copy.52
  66.4 0.1 copy.53
  66.5 0.1 select_reduce_fusion
  66.6 0.1 exponential_select_fusion
  66.7 0.1 mul.85
  66.8 0.1 mul.86
  66.9 4.5 %multiply_reduce_fusion = f32[512,128]{1,0:T(8,128)S(1)} fusion(bf16[32,520,128]{2,1,0:T(8,128)(2,1)} %bitcast.65, f32[32,512]{1,0:T(8,128)S(1)} %mul.86), kind=kLoop, calls=%fused_computation.1 | loop fusion | flops 6225920 | bytes 4521984 | tf_op jit(solution)/shard_map/reduce_sum | solution.py:62
  71.4 0.3 fusion.12
  71.7 0.8 multiply_reduce_fusion.1
  72.5 0.8 copy.49
  73.3 1.0 add_convert_fusion
  74.4 0.2 convolution_convert_fusion.1
  74.6 0.4 copy-done.1
  75.0 21.9 %all_to_all.10 = bf16[8,48,512]{2,1,0:T(8,128)(2,1)S(1)} all-to-all(bf16[8,48,512]{2,1,0:T(8,128)(2,1)S(1)} %convolution_convert_fusion.1), channel_id=1, replica_groups=mesh['ctx'=32,'exp'=8] {'exp'}, dimensions={0} | all-to-all | bytes 786432 | tf_op jit(solution)/shard_map/all_to_all | solution.py:114
  96.9 0.1 convert_bitcast_fusion
  97.0 0.1 copy.55
  97.1 0.2 fusion.14
  97.3 0.9 multiply_convert_fusion
  98.2 0.0 all-gather.4.cloned.1.call-update
  98.2 0.0 reduce-scatter.2.cloned.1.call-start
  98.3 62.5 %all-gather.4.cloned.1.call-done = bf16[1536,4096]{1,0:T(8,128)(2,1)} async-done(((bf16[48,4096]{1,0:T(8,128)(2,1)}), bf16[1536,4096]{1,0:T(8,128)(2,1)}) %all-gather.4.cloned.1.call-update) | async-done | bytes 12582928 | tf_op jit(solution)/shard_map/all_gather | solution.py:126
  160.8 11.5 %fusion.2 = f32[1536,384]{1,0:T(8,128)} fusion(bf16[1536,4096]{1,0:T(8,128)(2,1)} %all-gather.4.cloned.1.call-done, bf16[1,4096,384]{2,1,0:T(8,128)(2,1)} %param.27), kind=kOutput, calls=%fused_computation.5 | convolution fusion | flops 4831838208 | bytes 18087936 | tf_op jit(solution)/shard_map/dot_general | solution.py:127
  172.3 20.0 %convolution_convert_fusion = bf16[1536,4096]{1,0:T(8,128)(2,1)} fusion(bf16[1,384,4096]{2,1,0:T(8,128)(2,1)S(1)} %copy-done, bf16[1536,4096]{1,0:T(8,128)(2,1)} %all-gather.4.cloned.1.call-done, bf16[1,4096,384]{2,1,0:T(8,128)(2,1)} %param.28, f32[1536,384]{1,0:T(8,128)} %fusion.2), kind=kOutput, calls=%fused_computation | convolution fusion | flops 9673506816 | bytes 33816576 | tf_op jit(solution)/shard_map/dot_general | solution.py:130
  192.3 0.0 reduce-scatter.2.cloned.1.call-update
  192.4 111.2 %reduce-scatter.2.cloned.1.call-done = bf16[48,4096]{1,0:T(8,128)(2,1)} async-done(((bf16[1536,4096]{1,0:T(8,128)(2,1)}), bf16[48,4096]{1,0:T(8,128)(2,1)}) %reduce-scatter.2.cloned.1.call-update) | async-done | bytes 393232 | tf_op jit(solution)/shard_map/reduce_scatter | solution.py:133
  303.5 1.8 copy.57
  305.3 7.0 %all-to-all-start.1 = ((bf16[8,48,512]{2,1,0:T(8,128)(2,1)}), bf16[8,48,512]{2,1,0:T(8,128)(2,1)S(1)}, u32[]{:S(2)}, u32[]{:S(2)}) async-start(bf16[8,48,512]{2,1,0:T(8,128)(2,1)} %bitcast.67), calls=%async_computation.2 | async-start | bytes 786432 | tf_op jit(solution)/shard_map/all_to_all | solution.py:135
  312.3 0.7 select_reduce_fusion.1
  313.0 12.4 %all-to-all-done.1 = bf16[8,48,512]{2,1,0:T(8,128)(2,1)S(1)} async-done(((bf16[8,48,512]{2,1,0:T(8,128)(2,1)}), bf16[8,48,512]{2,1,0:T(8,128)(2,1)S(1)}, u32[]{:S(2)}, u32[]{:S(2)}) %all-to-all-start.1) | async-done | bytes 393248 | tf_op jit(solution)/shard_map/all_to_all | solution.py:135
  325.5 1.1 fusion.13
  (30 shorter events, 0.3 us)
Async XLA Ops:
  7.2 165.2 %copy-start = (bf16[1,384,4096]{2,1,0:T(8,128)(2,1)S(1)}, bf16[1,384,4096]{2,1,0:T(8,128)(2,1)}, u32[]{:S(2)}) copy-start(bf16[1,384,4096]{2,1,0:T(8,128)(2,1)} %param.29) | copy-start | bytes 9437188
  7.2 58.2 %all-gather.6.cloned.1.call-start = ((), (), s32[]{:S(2)}) async-start(), calls=%async_computation.5 | async-start | bytes 4392960 | tf_op jit(solution)/shard_map/all_gather | solution.py:48
  11.5 149.3 %all-gather.4.cloned.1.call-start = ((), (), s32[]{:S(2)}) async-start(), calls=%async_computation.3 | async-start | bytes 12976128 | tf_op jit(solution)/shard_map/all_gather | solution.py:126
  13.5 57.9 %copy-start.3 = (bf16[128,128]{1,0:T(8,128)(2,1)S(1)}, bf16[128,128]{1,0:T(8,128)(2,1)}, u32[]{:S(2)}) copy-start(bf16[128,128]{1,0:T(8,128)(2,1)} %param.21) | copy-start | bytes 98308
  66.9 4.8 %copy-start.2 = (f32[128,512]{0,1:T(8,128)S(1)}, f32[128,512]{0,1:T(8,128)}, u32[]{:S(2)}) copy-start(f32[128,512]{0,1:T(8,128)} %copy.48) | copy-start | bytes 786436
  66.9 4.8 %copy-start.4 = (f32[128,128]{1,0:T(8,128)S(1)}, f32[128,128]{1,0:T(8,128)}, u32[]{:S(2)}) copy-start(f32[128,128]{1,0:T(8,128)} %fusion.50) | copy-start | bytes 196612
  66.9 6.5 %copy-start.7 = (f32[512]{0:T(512)S(1)}, f32[512]{0:T(512)}, u32[]{:S(2)}) copy-start(f32[512]{0:T(512)} %param.24) | copy-start | bytes 6148
  72.5 24.8 %copy-start.5 = (f32[4096]{0:T(1024)S(1)}, f32[4096]{0:T(1024)}, u32[]{:S(2)}) copy-start(f32[4096]{0:T(1024)} %param.26) | copy-start | bytes 49156
  74.4 0.7 copy-start.1
  98.2 205.3 %reduce-scatter.2.cloned.1.call-start = ((), (), s32[]{:S(2)}) async-start(), calls=%async_computation.4 | async-start | bytes 12976128 | tf_op jit(solution)/shard_map/reduce_scatter | solution.py:133
  192.3 120.0 %copy-start.6 = (s32[128,2]{0,1:T(2,128)S(1)}, s32[128,2]{0,1:T(2,128)}, u32[]{:S(2)}) copy-start(s32[128,2]{0,1:T(2,128)} %param.30) | copy-start | bytes 3076
  305.3 20.1 %all-to-all-start.1 = ((bf16[8,48,512]{2,1,0:T(8,128)(2,1)}), bf16[8,48,512]{2,1,0:T(8,128)(2,1)S(1)}, u32[]{:S(2)}, u32[]{:S(2)}) async-start(bf16[8,48,512]{2,1,0:T(8,128)(2,1)} %bitcast.67), calls=%async_computation.2 | async-start | bytes 786432 | tf_op jit(solution)/shard_map/all_to_all | solution.py:135
Sparse Core Ops, SparseCore 0:
  11.6 53.7 all-gather.5
  98.3 62.4 all-gather.3
  192.5 111.0 reduce-scatter.1

commit v4 on v1

--- a/solution.py
+++ b/solution.py
@@ -40,34 +40,27 @@
 
 def carried_state(overall, states):
     head_count, head_width, nstate = states.shape
-    flat = states.astype(jnp.bfloat16).reshape(head_count * head_width, nstate)
+    rows = head_count * head_width
     high = overall.astype(jnp.bfloat16)
     low = (overall - high.astype(jnp.float32)).astype(jnp.bfloat16)
     extra = jnp.zeros((8, nstate), jnp.bfloat16)
     extra = extra.at[0, :head_count].set(high).at[1, :head_count].set(low)
-    packed = jnp.concatenate([flat, extra], axis=0)
-    chips = lax.axis_size("chip")
-    cores = lax.axis_size("core")
-    by_chip = lax.all_gather(packed, "chip")
-    everything = lax.all_gather(by_chip, "core")
-    shards = chips * cores
-    everything = everything.reshape(shards, packed.shape[0], nstate)
-    core_of = jnp.arange(shards, dtype=jnp.int32) // chips
-    chip_of = jnp.arange(shards, dtype=jnp.int32) % chips
-    shard_of = chip_of * cores + core_of
-    me = lax.axis_index("chip") * cores + lax.axis_index("core")
-    rows = head_count * head_width
+    packed = jnp.concatenate([states.astype(jnp.bfloat16).reshape(rows, nstate), extra], axis=0)
+    everything = lax.all_gather(packed, CTX)
+    shards = everything.shape[0]
+    me = lax.axis_index(CTX)
     decay_all = (
         everything[:, rows, :head_count].astype(jnp.float32)
         + everything[:, rows + 1, :head_count].astype(jnp.float32)
     )
+    shard_of = jnp.arange(shards, dtype=jnp.int32)
     between = (shard_of[:, None] < shard_of[None, :]) & (shard_of[None, :] < me)
     spans = jnp.sum(jnp.where(between[:, :, None], decay_all[None, :, :], 0.0), axis=1)
     weight = jnp.where((shard_of < me)[:, None], jnp.exp(spans), 0.0)
     gathered = everything[:, :rows, :].astype(jnp.float32).reshape(
         shards, head_count, head_width, nstate
     )
-    return jnp.einsum("kh,khpn->hpn", weight, gathered, precision=precise)
+    return jnp.sum(weight[:, :, None, None] * gathered, axis=0)
 
 
 def on_device(
@@ -131,21 +124,25 @@
     gate_here = gate_weight[0]
     up_here = up_weight[0]
     down_here = down_weight[0]
-    token_piece = lax.all_gather(
-        lax.all_gather(chosen, "chip", axis=0, tiled=True), "core", axis=0, tiled=True
-    )
+    token_piece = lax.all_gather(chosen, CTX, axis=0, tiled=True)
     gate_proj = jnp.dot(token_piece, gate_here, preferred_element_type=jnp.float32)
     up_proj = jnp.dot(token_piece, up_here, preferred_element_type=jnp.float32)
     hidden = (jax.nn.silu(gate_proj) * up_proj).astype(jnp.bfloat16)
-    partial_value = jnp.dot(hidden, down_here, preferred_element_type=jnp.float32).astype(
+    chips = lax.axis_size("chip")
+    core = lax.axis_index("core")
+    by_core = hidden.reshape(chips, 2, capacity, hidden.shape[-1])
+
+    def rows_of(which):
+        picked_rows = lax.dynamic_index_in_dim(by_core, which, 1, keepdims=False)
+        return picked_rows.reshape(chips * capacity, hidden.shape[-1])
+
+    other_part = jnp.dot(rows_of(1 - core), down_here, preferred_element_type=jnp.float32)
+    moved = lax.ppermute(other_part.astype(jnp.bfloat16), "core", [(0, 1), (1, 0)])
+    own_part = jnp.dot(rows_of(core), down_here, preferred_element_type=jnp.float32)
+    pair_sum = (own_part.astype(jnp.bfloat16).astype(jnp.float32) + moved.astype(jnp.float32)).astype(
         jnp.bfloat16
     )
-    summed = lax.psum_scatter(
-        lax.psum_scatter(partial_value, "core", scatter_dimension=0, tiled=True),
-        "chip",
-        scatter_dimension=0,
-        tiled=True,
-    )
+    summed = lax.psum_scatter(pair_sum, "chip", scatter_dimension=0, tiled=True)
     outgoing = jnp.transpose(summed.reshape(capacity, exp_count, channels), (1, 0, 2))
     returned = lax.all_to_all(outgoing, "exp", 0, 0)
     weights = tables * gate_sum[:, None, :]

time: 395 us -> 314 us (0.79)
  waiting for transfers between devices: 296 us -> 220 us
  matrix products: 39.4 us -> 32.1 us
  other arithmetic: 7.27 us -> 11.4 us
    all_gather x4 -> x2, waiting for transfers between devices: 164 us -> 112 us  [the longest x1 62.3 us: on_device(): token_piece = lax.all_gather(chosen, CTX, axis=0, tiled=True)]
    reduce_scatter x2 -> x1, waiting for transfers between devices: 120 us -> 86.1 us  [on_device(): summed = lax.psum_scatter(pair_sum, 'chip', scatter_dimension=0, tiled=True)]
    ppermute x0 -> x1, waiting for transfers between devices: none -> 9.91 us  [on_device(): lax.ppermute(other_part.astype(jnp.bfloat16), 'core', [(0, 1), (1, 0)])]
    dot_general x2 -> x3, matrix products: 23.5 us -> 16.2 us  [the longest x1 7.28 us: on_device(): up_proj = jnp.dot(token_piece, up_here, preferred_element_type=jnp.float32)]
    reduce_sum x0 -> x1, other arithmetic: none -> 4.46 us  [carried_state(): return jnp.sum(weight[:, :, None, None] * gathered, axis=0)]
  transfers between devices with their start and end apart: 7 -> 5, of which waited for: 7 -> 5; matrix products, arithmetic and copies ran while one was open for 1% -> 2% of each run, Pallas kernels for 0% -> 0%
where the time goes in v4:
time: 314 us
  waiting for transfers between devices  220 us (70%)
  matrix products  32.1 us (10%)
  blocking collectives  21.9 us (7%)
  between operations  14 us (4%)
  other arithmetic  11.4 us (4%)
  starting transfers between devices  7.68 us (2%)
  local copies, waits for them, and re-layouts  6.83 us (2%)
    reduce_scatter x1, waiting for transfers between devices, on_device(): summed = lax.psum_scatter(pair_sum, 'chip', scatter_dimension=0, tiled=True)  86.1 us
    all_gather x1, waiting for transfers between devices, on_device(): token_piece = lax.all_gather(chosen, CTX, axis=0, tiled=True)  62.3 us
    all_gather x1, waiting for transfers between devices, carried_state(): everything = lax.all_gather(packed, CTX)  49.3 us
    all_to_all x1, blocking collectives, on_device(): arrived = lax.all_to_all(picked, 'exp', 0, 0)  21.9 us
    all_to_all x1, waiting for transfers between devices, on_device(): returned = lax.all_to_all(outgoing, 'exp', 0, 0)  12.2 us
    dot_general x1, matrix products, on_device(): jnp.dot(token_piece, gate_here, preferred_element_type=jnp.float32)  11 us
    ppermute x1, waiting for transfers between devices, on_device(): lax.ppermute(other_part.astype(jnp.bfloat16), 'core', [(0, 1), (1, 0)])  9.91 us
    dot_general x1, matrix products, on_device(): up_proj = jnp.dot(token_piece, up_here, preferred_element_type=jnp.float32)  7.28 us
  transfers between devices with their start and end apart: 5, of which 5 were waited for; matrix products, arithmetic and copies ran while one was open for 2% of the time, Pallas kernels for 0%

profile of v4, /device:TPU:2, one launch (start us, length us, event | category | flops | bytes accessed | tf_op | source)
XLA Modules:
  0.0 313.8 jit_solution(12989381745325541604)
XLA Ops:
  7.2 0.9 negate_multiply_fusion
  8.1 0.1 copy.40
  8.2 0.2 reduce_window_sum.22
  8.5 1.0 copy.43
  9.6 1.0 convolution_convert_fusion.3
  10.6 0.2 scatter.9
  10.8 0.7 pad_maximum_fusion
  11.6 0.1 copy.44
  11.6 1.0 convert_multiply_fusion.1
  12.6 0.8 copy.48
  13.5 0.7 fusion.42
  14.2 0.3 reduce_window_sum.23
  14.5 1.6 fusion.47
  16.1 49.3 %all-gather.6.cloned.1.call-done = bf16[16640,128]{1,0:T(8,128)(2,1)} async-done(((bf16[520,128]{1,0:T(8,128)(2,1)}), bf16[16640,128]{1,0:T(8,128)(2,1)}) %all-gather.6.cloned.1.call-update) | async-done | bytes 4259856 | tf_op jit(solution)/shard_map/all_gather | solution.py:49
  65.3 0.9 fusion.45
  66.3 0.1 copy.52
  66.4 0.1 copy.53
  66.5 0.1 select_reduce_fusion
  66.6 0.1 exponential_select_fusion
  66.7 0.1 mul.89
  66.8 0.1 mul.90
  66.9 4.5 %multiply_reduce_fusion = f32[512,128]{1,0:T(8,128)S(1)} fusion(bf16[32,520,128]{2,1,0:T(8,128)(2,1)} %bitcast.70, f32[32,512]{1,0:T(8,128)S(1)} %mul.90), kind=kLoop, calls=%fused_computation.1 | loop fusion | flops 6225920 | bytes 4521984 | tf_op jit(solution)/shard_map/reduce_sum | solution.py:63
  71.4 0.3 fusion.10
  71.7 0.8 multiply_reduce_fusion.1
  72.5 0.8 copy.49
  73.3 1.0 add_convert_fusion.1
  74.4 0.2 convolution_convert_fusion.2
  74.6 0.4 copy-done.1
  75.0 21.9 %all_to_all.10 = bf16[8,48,512]{2,1,0:T(8,128)(2,1)S(1)} all-to-all(bf16[8,48,512]{2,1,0:T(8,128)(2,1)S(1)} %convolution_convert_fusion.2), channel_id=1, replica_groups=mesh['chip'=16,'core'=2,'exp'=8] {'exp'}, dimensions={0} | all-to-all | bytes 786432 | tf_op jit(solution)/shard_map/all_to_all | solution.py:115
  96.9 0.1 convert_bitcast_fusion
  97.0 0.1 copy.55
  97.1 0.2 fusion.12
  97.3 0.9 multiply_convert_fusion
  98.2 0.2 reduce-scatter.2.cloned.1.call-start
  98.4 62.3 %all-gather.4.cloned.1.call-done = bf16[1536,4096]{1,0:T(8,128)(2,1)} async-done(((bf16[48,4096]{1,0:T(8,128)(2,1)}), bf16[1536,4096]{1,0:T(8,128)(2,1)}) %all-gather.4.cloned.1.call-update) | async-done | bytes 12582928 | tf_op jit(solution)/shard_map/all_gather | solution.py:127
  160.8 11.0 %fusion.3 = f32[1536,384]{1,0:T(8,128)S(1)} fusion(bf16[1536,4096]{1,0:T(8,128)(2,1)} %all-gather.4.cloned.1.call-done, bf16[1,4096,384]{2,1,0:T(8,128)(2,1)} %param.27), kind=kOutput, calls=%fused_computation.8 | convolution fusion | flops 4831838208 | bytes 18087936 | tf_op jit(solution)/shard_map/dot_general | solution.py:128
  171.8 7.3 %fusion.5 = bf16[1536,384]{1,0:T(8,128)(2,1)S(1)} fusion(bf16[1536,4096]{1,0:T(8,128)(2,1)S(1)} %copy-done.8, bf16[1,4096,384]{2,1,0:T(8,128)(2,1)S(1)} %copy-done.9, f32[1536,384]{1,0:T(8,128)S(1)} %fusion.3), kind=kOutput, calls=%fused_computation.10 | convolution fusion | flops 4835377152 | bytes 19267584 | tf_op jit(solution)/shard_map/dot_general | solution.py:129
  179.1 0.1 constant_dynamic-slice_fusion.1
  179.2 3.7 %convolution_convert_fusion = bf16[768,4096]{1,0:T(8,128)(2,1)S(1)} fusion(bf16[768,384]{1,0:T(8,128)(2,1)S(1)} %bitcast.77, bf16[1,384,4096]{2,1,0:T(8,128)(2,1)S(1)} %copy-done), kind=kOutput, calls=%fused_computation.2 | convolution fusion | flops 2419064832 | bytes 10027008 | tf_op jit(solution)/shard_map/dot_general | solution.py:139
  182.9 0.3 collective-permute-start
  183.2 9.9 %collective-permute-done = bf16[768,4096]{1,0:T(8,128)(2,1)S(1)} collective-permute-done((bf16[768,4096]{1,0:T(8,128)(2,1)S(1)}, bf16[768,4096]{1,0:T(8,128)(2,1)S(1)}, u32[]{:S(2)}, u32[]{:S(2)}) %collective-permute-start) | collective-permute-done | bytes 6291488 | tf_op jit(solution)/shard_map/ppermute | solution.py:140
  193.1 5.3 %add_convert_fusion = bf16[768,4096]{1,0:T(8,128)(2,1)} fusion(bf16[768,4096]{1,0:T(8,128)(2,1)S(1)} %collective-permute-done, bf16[768,384]{1,0:T(8,128)(2,1)S(1)} %bitcast.76, bf16[1,384,4096]{2,1,0:T(8,128)(2,1)S(1)} %copy-done), kind=kOutput, calls=%fused_computation | convolution fusion | flops 2431647744 | bytes 16318464 | tf_op jit(solution)/shard_map/dot_general | solution.py:141
  198.4 86.1 %reduce-scatter.2.cloned.1.call-done = bf16[48,4096]{1,0:T(8,128)(2,1)} async-done(((bf16[768,4096]{1,0:T(8,128)(2,1)}), bf16[48,4096]{1,0:T(8,128)(2,1)}) %reduce-scatter.2.cloned.1.call-update) | async-done | bytes 393232 | tf_op jit(solution)/shard_map/reduce_scatter | solution.py:145
  284.4 1.8 copy.57
  286.2 7.0 %all-to-all-start.1 = ((bf16[8,48,512]{2,1,0:T(8,128)(2,1)}), bf16[8,48,512]{2,1,0:T(8,128)(2,1)S(1)}, u32[]{:S(2)}, u32[]{:S(2)}) async-start(bf16[8,48,512]{2,1,0:T(8,128)(2,1)} %bitcast.72), calls=%async_computation.2 | async-start | bytes 786432 | tf_op jit(solution)/shard_map/all_to_all | solution.py:147
  293.3 0.7 select_reduce_fusion.1
  294.0 12.2 %all-to-all-done.1 = bf16[8,48,512]{2,1,0:T(8,128)(2,1)S(1)} async-done(((bf16[8,48,512]{2,1,0:T(8,128)(2,1)}), bf16[8,48,512]{2,1,0:T(8,128)(2,1)S(1)}, u32[]{:S(2)}, u32[]{:S(2)}) %all-to-all-start.1) | async-done | bytes 393248 | tf_op jit(solution)/shard_map/all_to_all | solution.py:147
  306.2 1.1 fusion.11
  (39 shorter events, 0.4 us)
Async XLA Ops:
  7.2 172.0 %copy-start = (bf16[1,384,4096]{2,1,0:T(8,128)(2,1)S(1)}, bf16[1,384,4096]{2,1,0:T(8,128)(2,1)}, u32[]{:S(2)}) copy-start(bf16[1,384,4096]{2,1,0:T(8,128)(2,1)} %param.29) | copy-start | bytes 9437188
  7.2 58.2 %all-gather.6.cloned.1.call-start = ((), (), s32[]{:S(2)}) async-start(), calls=%async_computation.5 | async-start | bytes 4392960 | tf_op jit(solution)/shard_map/all_gather | solution.py:49
  11.4 149.3 %all-gather.4.cloned.1.call-start = ((), (), s32[]{:S(2)}) async-start(), calls=%async_computation.3 | async-start | bytes 12976128 | tf_op jit(solution)/shard_map/all_gather | solution.py:127
  13.5 57.9 %copy-start.3 = (bf16[128,128]{1,0:T(8,128)(2,1)S(1)}, bf16[128,128]{1,0:T(8,128)(2,1)}, u32[]{:S(2)}) copy-start(bf16[128,128]{1,0:T(8,128)(2,1)} %param.21) | copy-start | bytes 98308
  66.8 4.8 %copy-start.2 = (f32[128,512]{0,1:T(8,128)S(1)}, f32[128,512]{0,1:T(8,128)}, u32[]{:S(2)}) copy-start(f32[128,512]{0,1:T(8,128)} %copy.48) | copy-start | bytes 786436
  66.9 4.8 %copy-start.4 = (f32[128,128]{1,0:T(8,128)S(1)}, f32[128,128]{1,0:T(8,128)}, u32[]{:S(2)}) copy-start(f32[128,128]{1,0:T(8,128)} %fusion.47) | copy-start | bytes 196612
  66.9 6.5 %copy-start.7 = (f32[512]{0:T(512)S(1)}, f32[512]{0:T(512)}, u32[]{:S(2)}) copy-start(f32[512]{0:T(512)} %param.24) | copy-start | bytes 6148
  72.5 24.8 %copy-start.5 = (f32[4096]{0:T(1024)S(1)}, f32[4096]{0:T(1024)}, u32[]{:S(2)}) copy-start(f32[4096]{0:T(1024)} %param.26) | copy-start | bytes 49156
  74.4 0.7 copy-start.1
  98.2 186.3 %reduce-scatter.2.cloned.1.call-start = ((), (), s32[]{:S(2)}) async-start(), calls=%async_computation.4 | async-start | bytes 6684672 | tf_op jit(solution)/shard_map/reduce_scatter | solution.py:145
  160.8 11.0 %copy-start.8 = (bf16[1536,4096]{1,0:T(8,128)(2,1)S(1)}, bf16[1536,4096]{1,0:T(8,128)(2,1)}, u32[]{:S(2)}) copy-start(bf16[1536,4096]{1,0:T(8,128)(2,1)} %all-gather.4.cloned.1.call-done) | copy-start | bytes 37748740
  160.8 11.0 %copy-start.9 = (bf16[1,4096,384]{2,1,0:T(8,128)(2,1)S(1)}, bf16[1,4096,384]{2,1,0:T(8,128)(2,1)}, u32[]{:S(2)}) copy-start(bf16[1,4096,384]{2,1,0:T(8,128)(2,1)} %param.28) | copy-start | bytes 9437188
  182.9 10.2 %collective-permute-start = (bf16[768,4096]{1,0:T(8,128)(2,1)S(1)}, bf16[768,4096]{1,0:T(8,128)(2,1)S(1)}, u32[]{:S(2)}, u32[]{:S(2)}) collective-permute-start(bf16[768,4096]{1,0:T(8,128)(2,1)S(1)} %convolution_convert_fusion), channel_id=1, source_target_pairs={{0,8},{8,0},{1,9},{9,1},{2,10},{10,2},{3,11},{11,3},{4,12},{12,4},... | collective-permute-start | bytes 18874376 | tf_op jit(solution)/shard_map/ppermute | solution.py:140
  198.4 94.9 %copy-start.6 = (s32[128,2]{0,1:T(2,128)S(1)}, s32[128,2]{0,1:T(2,128)}, u32[]{:S(2)}) copy-start(s32[128,2]{0,1:T(2,128)} %param.30) | copy-start | bytes 3076
  286.2 20.0 %all-to-all-start.1 = ((bf16[8,48,512]{2,1,0:T(8,128)(2,1)}), bf16[8,48,512]{2,1,0:T(8,128)(2,1)S(1)}, u32[]{:S(2)}, u32[]{:S(2)}) async-start(bf16[8,48,512]{2,1,0:T(8,128)(2,1)} %bitcast.72), calls=%async_computation.2 | async-start | bytes 786432 | tf_op jit(solution)/shard_map/all_to_all | solution.py:147
Sparse Core Ops, SparseCore 0:
  11.6 53.7 all-gather.5
  98.3 62.4 all-gather.3
  198.5 85.8 reduce-scatter.1

commit v5 on v4

--- a/solution.py
+++ b/solution.py
@@ -139,9 +139,8 @@
     other_part = jnp.dot(rows_of(1 - core), down_here, preferred_element_type=jnp.float32)
     moved = lax.ppermute(other_part.astype(jnp.bfloat16), "core", [(0, 1), (1, 0)])
     own_part = jnp.dot(rows_of(core), down_here, preferred_element_type=jnp.float32)
-    pair_sum = (own_part.astype(jnp.bfloat16).astype(jnp.float32) + moved.astype(jnp.float32)).astype(
-        jnp.bfloat16
-    )
+    own_part = lax.optimization_barrier(own_part.astype(jnp.bfloat16))
+    pair_sum = (own_part.astype(jnp.float32) + moved.astype(jnp.float32)).astype(jnp.bfloat16)
     summed = lax.psum_scatter(pair_sum, "chip", scatter_dimension=0, tiled=True)
     outgoing = jnp.transpose(summed.reshape(capacity, exp_count, channels), (1, 0, 2))
     returned = lax.all_to_all(outgoing, "exp", 0, 0)

time: 314 us -> 320 us (1.019)
  other arithmetic: 11.4 us -> 22.4 us
  waiting for transfers between devices: 220 us -> 214 us
    convert_element_type x0 -> x1, other arithmetic: none -> 10.4 us  [on_device(): (own_part.astype(jnp.float32) + moved.astype(jnp.float32)).astype(jnp.bfl...]
    ppermute x1, waiting for transfers between devices: 9.91 us -> 4.78 us  [on_device(): lax.ppermute(other_part.astype(jnp.bfloat16), 'core', [(0, 1), (1, 0)])]
  transfers between devices with their start and end apart: 5 -> 5, of which waited for: 5 -> 5; matrix products, arithmetic and copies ran while one was open for 2% -> 3% of each run, Pallas kernels for 0% -> 0%
where the time goes in v5:
time: 320 us
  waiting for transfers between devices  214 us (67%)
  matrix products  32.1 us (10%)
  other arithmetic  22.4 us (7%)
  blocking collectives  21.9 us (7%)
  between operations  14 us (4%)
  starting transfers between devices  7.87 us (2%)
  local copies, waits for them, and re-layouts  6.82 us (2%)
    reduce_scatter x1, waiting for transfers between devices, on_device(): summed = lax.psum_scatter(pair_sum, 'chip', scatter_dimension=0, tiled=True)  86.1 us
    all_gather x1, waiting for transfers between devices, on_device(): token_piece = lax.all_gather(chosen, CTX, axis=0, tiled=True)  62.3 us
    all_gather x1, waiting for transfers between devices, carried_state(): everything = lax.all_gather(packed, CTX)  48.7 us
    all_to_all x1, blocking collectives, on_device(): arrived = lax.all_to_all(picked, 'exp', 0, 0)  21.9 us
    all_to_all x1, waiting for transfers between devices, on_device(): returned = lax.all_to_all(outgoing, 'exp', 0, 0)  12.4 us
    dot_general x1, matrix products, on_device(): jnp.dot(token_piece, gate_here, preferred_element_type=jnp.float32)  11 us
    convert_element_type x1, other arithmetic, on_device(): (own_part.astype(jnp.float32) + moved.astype(jnp.float32)).astype(jnp.bfl...  10.4 us
    dot_general x1, matrix products, on_device(): up_proj = jnp.dot(token_piece, up_here, preferred_element_type=jnp.float32)  7.28 us
  transfers between devices with their start and end apart: 5, of which 5 were waited for; matrix products, arithmetic and copies ran while one was open for 3% of the time, Pallas kernels for 0%

profile of v5, /device:TPU:2, one launch (start us, length us, event | category | flops | bytes accessed | tf_op | source)
XLA Modules:
  0.0 319.5 jit_solution(12504154805638215686)
XLA Ops:
  7.2 0.9 negate_multiply_fusion
  8.1 0.1 copy.40
  8.2 0.2 reduce_window_sum.22
  8.5 1.0 copy.43
  9.6 1.0 convolution_convert_fusion.3
  10.6 0.2 scatter.9
  10.8 0.7 pad_maximum_fusion
  11.6 1.0 convert_multiply_fusion.1
  12.6 0.8 copy.48
  13.5 0.7 fusion.42
  14.2 0.3 reduce_window_sum.23
  14.4 0.6 iota_compare_fusion.1
  15.1 1.6 fusion.47
  16.6 48.7 %all-gather.6.cloned.1.call-done = bf16[16640,128]{1,0:T(8,128)(2,1)} async-done(((bf16[520,128]{1,0:T(8,128)(2,1)}), bf16[16640,128]{1,0:T(8,128)(2,1)}) %all-gather.6.cloned.1.call-update) | async-done | bytes 4259856 | tf_op jit(solution)/shard_map/all_gather | solution.py:49
  65.3 0.9 fusion.45
  66.3 0.1 copy.52
  66.4 0.1 copy.53
  66.5 0.1 select_reduce_fusion
  66.6 0.1 exponential_select_fusion
  66.7 0.1 mul.89
  66.8 0.1 mul.90
  66.9 4.5 %multiply_reduce_fusion = f32[512,128]{1,0:T(8,128)S(1)} fusion(bf16[32,520,128]{2,1,0:T(8,128)(2,1)} %bitcast.70, f32[32,512]{1,0:T(8,128)S(1)} %mul.90), kind=kLoop, calls=%fused_computation.1 | loop fusion | flops 6225920 | bytes 4521984 | tf_op jit(solution)/shard_map/reduce_sum | solution.py:63
  71.4 0.3 fusion.10
  71.7 0.8 multiply_reduce_fusion.1
  72.5 0.8 copy.49
  73.3 1.1 add_convert_fusion.1
  74.4 0.2 convolution_convert_fusion.2
  74.7 0.4 copy-done.1
  75.1 21.9 %all_to_all.10 = bf16[8,48,512]{2,1,0:T(8,128)(2,1)S(1)} all-to-all(bf16[8,48,512]{2,1,0:T(8,128)(2,1)S(1)} %convolution_convert_fusion.2), channel_id=1, replica_groups=mesh['chip'=16,'core'=2,'exp'=8] {'exp'}, dimensions={0} | all-to-all | bytes 786432 | tf_op jit(solution)/shard_map/all_to_all | solution.py:115
  96.9 0.1 convert_bitcast_fusion
  97.1 0.2 fusion.12
  97.3 0.9 multiply_convert_fusion
  98.2 0.2 reduce-scatter.2.cloned.1.call-start
  98.5 62.3 %all-gather.4.cloned.1.call-done = bf16[1536,4096]{1,0:T(8,128)(2,1)} async-done(((bf16[48,4096]{1,0:T(8,128)(2,1)}), bf16[1536,4096]{1,0:T(8,128)(2,1)}) %all-gather.4.cloned.1.call-update) | async-done | bytes 12582928 | tf_op jit(solution)/shard_map/all_gather | solution.py:127
  160.8 11.0 %fusion.3 = f32[1536,384]{1,0:T(8,128)S(1)} fusion(bf16[1536,4096]{1,0:T(8,128)(2,1)} %all-gather.4.cloned.1.call-done, bf16[1,4096,384]{2,1,0:T(8,128)(2,1)} %param.27), kind=kOutput, calls=%fused_computation.8 | convolution fusion | flops 4831838208 | bytes 18087936 | tf_op jit(solution)/shard_map/dot_general | solution.py:128
  171.8 7.3 %fusion.5 = bf16[1536,384]{1,0:T(8,128)(2,1)S(1)} fusion(bf16[1536,4096]{1,0:T(8,128)(2,1)S(1)} %copy-done.8, bf16[1,4096,384]{2,1,0:T(8,128)(2,1)S(1)} %copy-done.9, f32[1536,384]{1,0:T(8,128)S(1)} %fusion.3), kind=kOutput, calls=%fused_computation.10 | convolution fusion | flops 4835377152 | bytes 19267584 | tf_op jit(solution)/shard_map/dot_general | solution.py:129
  179.1 0.1 constant_dynamic-slice_fusion.1
  179.2 3.7 %convolution_convert_fusion = bf16[768,4096]{1,0:T(8,128)(2,1)S(1)} fusion(bf16[768,384]{1,0:T(8,128)(2,1)S(1)} %bitcast.77, bf16[1,384,4096]{2,1,0:T(8,128)(2,1)S(1)} %copy-done), kind=kOutput, calls=%fused_computation.2 | convolution fusion | flops 2419064832 | bytes 10027008 | tf_op jit(solution)/shard_map/dot_general | solution.py:139
  182.9 0.6 collective-permute-start
  183.5 5.3 %convolution_convert_fusion.1 = bf16[768,4096]{1,0:T(8,128)(2,1)} fusion(bf16[768,384]{1,0:T(8,128)(2,1)S(1)} %bitcast.76, bf16[1,384,4096]{2,1,0:T(8,128)(2,1)S(1)} %copy-done), kind=kOutput, calls=%fused_computation.3 | convolution fusion | flops 2419064832 | bytes 10027008 | tf_op jit(solution)/shard_map/dot_general | solution.py:141
  188.7 4.8 %collective-permute-done = bf16[768,4096]{1,0:T(8,128)(2,1)} collective-permute-done((bf16[768,4096]{1,0:T(8,128)(2,1)S(1)}, bf16[768,4096]{1,0:T(8,128)(2,1)}, u32[]{:S(2)}, u32[]{:S(2)}) %collective-permute-start) | collective-permute-done | bytes 6291488 | tf_op jit(solution)/shard_map/ppermute | solution.py:140
  193.5 10.4 %add_convert_fusion = bf16[768,4096]{1,0:T(8,128)(2,1)} fusion(bf16[768,4096]{1,0:T(8,128)(2,1)} %collective-permute-done, bf16[768,4096]{1,0:T(8,128)(2,1)} %convolution_convert_fusion.1), kind=kLoop, calls=%fused_computation | loop fusion | flops 12582912 | bytes 18874368 | tf_op jit(solution)/shard_map/convert_element_type | solution.py:143
  203.9 86.1 %reduce-scatter.2.cloned.1.call-done = bf16[48,4096]{1,0:T(8,128)(2,1)} async-done(((bf16[768,4096]{1,0:T(8,128)(2,1)}), bf16[48,4096]{1,0:T(8,128)(2,1)}) %reduce-scatter.2.cloned.1.call-update) | async-done | bytes 393232 | tf_op jit(solution)/shard_map/reduce_scatter | solution.py:144
  290.0 1.8 copy.57
  291.8 7.0 %all-to-all-start.1 = ((bf16[8,48,512]{2,1,0:T(8,128)(2,1)}), bf16[8,48,512]{2,1,0:T(8,128)(2,1)S(1)}, u32[]{:S(2)}, u32[]{:S(2)}) async-start(bf16[8,48,512]{2,1,0:T(8,128)(2,1)} %bitcast.72), calls=%async_computation.2 | async-start | bytes 786432 | tf_op jit(solution)/shard_map/all_to_all | solution.py:146
  298.8 0.7 select_reduce_fusion.1
  299.5 12.4 %all-to-all-done.1 = bf16[8,48,512]{2,1,0:T(8,128)(2,1)S(1)} async-done(((bf16[8,48,512]{2,1,0:T(8,128)(2,1)}), bf16[8,48,512]{2,1,0:T(8,128)(2,1)S(1)}, u32[]{:S(2)}, u32[]{:S(2)}) %all-to-all-start.1) | async-done | bytes 393248 | tf_op jit(solution)/shard_map/all_to_all | solution.py:146
  311.9 1.1 fusion.11
  (40 shorter events, 0.5 us)
Async XLA Ops:
  7.2 172.1 %copy-start = (bf16[1,384,4096]{2,1,0:T(8,128)(2,1)S(1)}, bf16[1,384,4096]{2,1,0:T(8,128)(2,1)}, u32[]{:S(2)}) copy-start(bf16[1,384,4096]{2,1,0:T(8,128)(2,1)} %param.29) | copy-start | bytes 9437188
  7.2 58.2 %all-gather.6.cloned.1.call-start = ((), (), s32[]{:S(2)}) async-start(), calls=%async_computation.5 | async-start | bytes 4392960 | tf_op jit(solution)/shard_map/all_gather | solution.py:49
  11.4 149.4 %all-gather.4.cloned.1.call-start = ((), (), s32[]{:S(2)}) async-start(), calls=%async_computation.3 | async-start | bytes 12976128 | tf_op jit(solution)/shard_map/all_gather | solution.py:127
  13.5 57.9 %copy-start.3 = (bf16[128,128]{1,0:T(8,128)(2,1)S(1)}, bf16[128,128]{1,0:T(8,128)(2,1)}, u32[]{:S(2)}) copy-start(bf16[128,128]{1,0:T(8,128)(2,1)} %param.21) | copy-start | bytes 98308
  66.7 5.0 %copy-start.6 = (pred[128,128]{1,0:T(8,128)(4,1)S(1)}, pred[128,128]{1,0:T(8,128)(4,1)}, u32[]{:S(2)}) copy-start(pred[128,128]{1,0:T(8,128)(4,1)} %iota_compare_fusion.1) | copy-start | bytes 49156
  66.9 4.8 %copy-start.2 = (f32[128,512]{0,1:T(8,128)S(1)}, f32[128,512]{0,1:T(8,128)}, u32[]{:S(2)}) copy-start(f32[128,512]{0,1:T(8,128)} %copy.48) | copy-start | bytes 786436
  66.9 4.8 %copy-start.4 = (f32[128,128]{1,0:T(8,128)S(1)}, f32[128,128]{1,0:T(8,128)}, u32[]{:S(2)}) copy-start(f32[128,128]{1,0:T(8,128)} %fusion.47) | copy-start | bytes 196612
  72.5 24.8 %copy-start.5 = (f32[4096]{0:T(1024)S(1)}, f32[4096]{0:T(1024)}, u32[]{:S(2)}) copy-start(f32[4096]{0:T(1024)} %param.26) | copy-start | bytes 49156
  74.4 0.7 copy-start.1
  98.2 191.8 %reduce-scatter.2.cloned.1.call-start = ((), (), s32[]{:S(2)}) async-start(), calls=%async_computation.4 | async-start | bytes 6684672 | tf_op jit(solution)/shard_map/reduce_scatter | solution.py:144
  160.8 11.0 %copy-start.8 = (bf16[1536,4096]{1,0:T(8,128)(2,1)S(1)}, bf16[1536,4096]{1,0:T(8,128)(2,1)}, u32[]{:S(2)}) copy-start(bf16[1536,4096]{1,0:T(8,128)(2,1)} %all-gather.4.cloned.1.call-done) | copy-start | bytes 37748740
  160.8 11.0 %copy-start.9 = (bf16[1,4096,384]{2,1,0:T(8,128)(2,1)S(1)}, bf16[1,4096,384]{2,1,0:T(8,128)(2,1)}, u32[]{:S(2)}) copy-start(bf16[1,4096,384]{2,1,0:T(8,128)(2,1)} %param.28) | copy-start | bytes 9437188
  182.9 10.6 %collective-permute-start = (bf16[768,4096]{1,0:T(8,128)(2,1)S(1)}, bf16[768,4096]{1,0:T(8,128)(2,1)}, u32[]{:S(2)}, u32[]{:S(2)}) collective-permute-start(bf16[768,4096]{1,0:T(8,128)(2,1)S(1)} %convolution_convert_fusion), channel_id=1, source_target_pairs={{0,8},{8,0},{1,9},{9,1},{2,10},{10,2},{3,11},{11,3},{4,12},{12,4},... | collective-permute-start | bytes 18874376 | tf_op jit(solution)/shard_map/ppermute | solution.py:140
  203.9 94.9 %copy-start.7 = (s32[128,2]{0,1:T(2,128)S(1)}, s32[128,2]{0,1:T(2,128)}, u32[]{:S(2)}) copy-start(s32[128,2]{0,1:T(2,128)} %param.30) | copy-start | bytes 3076
  291.8 20.1 %all-to-all-start.1 = ((bf16[8,48,512]{2,1,0:T(8,128)(2,1)}), bf16[8,48,512]{2,1,0:T(8,128)(2,1)S(1)}, u32[]{:S(2)}, u32[]{:S(2)}) async-start(bf16[8,48,512]{2,1,0:T(8,128)(2,1)} %bitcast.72), calls=%async_computation.2 | async-start | bytes 786432 | tf_op jit(solution)/shard_map/all_to_all | solution.py:146
Sparse Core Ops, SparseCore 0:
  11.6 53.7 all-gather.5
  98.3 62.4 all-gather.3
  204.0 85.9 reduce-scatter.1

commit v6 on v4

--- a/solution.py
+++ b/solution.py
@@ -124,21 +124,19 @@
     gate_here = gate_weight[0]
     up_here = up_weight[0]
     down_here = down_weight[0]
-    token_piece = lax.all_gather(chosen, CTX, axis=0, tiled=True)
-    gate_proj = jnp.dot(token_piece, gate_here, preferred_element_type=jnp.float32)
-    up_proj = jnp.dot(token_piece, up_here, preferred_element_type=jnp.float32)
-    hidden = (jax.nn.silu(gate_proj) * up_proj).astype(jnp.bfloat16)
-    chips = lax.axis_size("chip")
+    token_piece = lax.all_gather(chosen, ("core", "chip"), axis=0, tiled=True)
     core = lax.axis_index("core")
-    by_core = hidden.reshape(chips, 2, capacity, hidden.shape[-1])
+    half = token_piece.shape[0] // lax.axis_size("core")
 
-    def rows_of(which):
-        picked_rows = lax.dynamic_index_in_dim(by_core, which, 1, keepdims=False)
-        return picked_rows.reshape(chips * capacity, hidden.shape[-1])
+    def expert_rows(which):
+        rows = lax.dynamic_slice_in_dim(token_piece, which * half, half, 0)
+        gate_proj = jnp.dot(rows, gate_here, preferred_element_type=jnp.float32)
+        up_proj = jnp.dot(rows, up_here, preferred_element_type=jnp.float32)
+        hidden = (jax.nn.silu(gate_proj) * up_proj).astype(jnp.bfloat16)
+        return jnp.dot(hidden, down_here, preferred_element_type=jnp.float32)
 
-    other_part = jnp.dot(rows_of(1 - core), down_here, preferred_element_type=jnp.float32)
-    moved = lax.ppermute(other_part.astype(jnp.bfloat16), "core", [(0, 1), (1, 0)])
-    own_part = jnp.dot(rows_of(core), down_here, preferred_element_type=jnp.float32)
+    moved = lax.ppermute(expert_rows(1 - core).astype(jnp.bfloat16), "core", [(0, 1), (1, 0)])
+    own_part = expert_rows(core)
     pair_sum = (own_part.astype(jnp.bfloat16).astype(jnp.float32) + moved.astype(jnp.float32)).astype(
         jnp.bfloat16
     )

time: 314 us -> 316 us (level)
  waiting for transfers between devices: 220 us -> 209 us
  matrix products: 32.1 us -> 41.3 us
    ppermute x1, waiting for transfers between devices: 9.91 us -> 0.01 us  [on_device(): lax.ppermute(expert_rows(1 - core).astype(jnp.bfloat16), 'core', [(0, 1),...]
    dot_general x4 -> x6, matrix products: 27.2 us -> 35.6 us  [the longest x2 13.1 us: expert_rows(): gate_proj = jnp.dot(rows, gate_here, preferred_element_type=jnp.float32)]
  transfers between devices with their start and end apart: 5 -> 5, of which waited for: 5 -> 4; matrix products, arithmetic and copies ran while one was open for 2% -> 6% of each run, Pallas kernels for 0% -> 0%
where the time goes in v6:
time: 316 us; the launch traced here: 315 us
  waiting for transfers between devices  209 us (66%)
  matrix products  41.3 us (13%)
  blocking collectives  21.9 us (7%)
  between operations  14 us (4%)
  other arithmetic  12 us (4%)
  local copies, waits for them, and re-layouts  9.2 us (3%)
  starting transfers between devices  7.36 us (2%)
    reduce_scatter x1, waiting for transfers between devices, on_device(): summed = lax.psum_scatter(pair_sum, 'chip', scatter_dimension=0, tiled=True)  86.2 us
    all_gather x1, waiting for transfers between devices, on_device(): token_piece = lax.all_gather(chosen, ('core', 'chip'), axis=0, tiled=True)  62.5 us
    all_gather x1, waiting for transfers between devices, carried_state(): everything = lax.all_gather(packed, CTX)  48.2 us
    all_to_all x1, blocking collectives, on_device(): arrived = lax.all_to_all(picked, 'exp', 0, 0)  21.9 us
    dot_general x2, matrix products, expert_rows(): gate_proj = jnp.dot(rows, gate_here, preferred_element_type=jnp.float32)  13.1 us
    dot_general x2, matrix products, expert_rows(): return jnp.dot(hidden, down_here, preferred_element_type=jnp.float32)  12.7 us
    all_to_all x1, waiting for transfers between devices, on_device(): returned = lax.all_to_all(outgoing, 'exp', 0, 0)  12.3 us
    dot_general x2, matrix products, expert_rows(): up_proj = jnp.dot(rows, up_here, preferred_element_type=jnp.float32)  9.75 us
  transfers between devices with their start and end apart: 5, of which 4 were waited for; matrix products, arithmetic and copies ran while one was open for 6% of the time, Pallas kernels for 0%

profile of v6, /device:TPU:2, one launch (start us, length us, event | category | flops | bytes accessed | tf_op | source)
XLA Modules:
  0.0 315.0 jit_solution(17309650210692663449)
XLA Ops:
  7.2 0.9 negate_multiply_fusion
  8.1 0.1 copy.40
  8.2 0.2 reduce_window_sum.22
  8.5 1.0 copy.43
  9.6 1.0 convolution_convert_fusion.3
  10.6 0.2 scatter.9
  10.8 0.7 pad_maximum_fusion
  11.5 0.7 copy.41
  12.2 0.7 fusion.68
  12.9 0.3 reduce_window_sum.23
  13.2 1.0 convert_multiply_fusion.1
  14.2 0.8 copy.48
  15.1 0.6 iota_compare_fusion.1
  15.7 1.6 fusion.77
  17.2 48.2 %all-gather.6.cloned.1.call-done = bf16[16640,128]{1,0:T(8,128)(2,1)} async-done(((bf16[520,128]{1,0:T(8,128)(2,1)}), bf16[16640,128]{1,0:T(8,128)(2,1)}) %all-gather.6.cloned.1.call-update) | async-done | bytes 4259856 | tf_op jit(solution)/shard_map/all_gather | solution.py:49
  65.4 0.9 fusion.75
  66.4 0.1 copy.52
  66.4 0.1 copy.53
  66.5 0.1 select_reduce_fusion
  66.7 0.1 mul.101
  66.8 0.1 mul.102
  67.0 4.5 %multiply_reduce_fusion = f32[512,128]{1,0:T(8,128)S(1)} fusion(bf16[32,520,128]{2,1,0:T(8,128)(2,1)} %bitcast.75, f32[32,512]{1,0:T(8,128)S(1)} %mul.102), kind=kLoop, calls=%fused_computation.1 | loop fusion | flops 6225920 | bytes 4521984 | tf_op jit(solution)/shard_map/reduce_sum | solution.py:63
  71.4 0.3 fusion.36
  71.8 1.5 multiply_reduce_fusion.1
  73.3 0.8 copy.49
  74.2 1.0 add_convert_fusion.1
  75.2 0.6 copy-done.1
  75.9 0.2 convolution_convert_fusion.2
  76.1 21.9 %all_to_all.10 = bf16[8,48,512]{2,1,0:T(8,128)(2,1)S(1)} all-to-all(bf16[8,48,512]{2,1,0:T(8,128)(2,1)S(1)} %convolution_convert_fusion.2), channel_id=1, replica_groups=mesh['chip'=16,'core'=2,'exp'=8] {'exp'}, dimensions={0} | all-to-all | bytes 786432 | tf_op jit(solution)/shard_map/all_to_all | solution.py:115
  98.0 0.2 fusion.38
  98.2 0.1 convert_bitcast_fusion
  98.4 0.9 multiply_convert_fusion
  99.3 62.5 %all-gather.4.cloned.1.call-done = bf16[1536,4096]{1,0:T(8,128)(2,1)} async-done(((bf16[48,4096]{1,0:T(8,128)(2,1)}), bf16[1536,4096]{1,0:T(8,128)(2,1)}) %all-gather.4.cloned.1.call-update) | async-done | bytes 12582928 | tf_op jit(solution)/shard_map/all_gather | solution.py:127
  161.9 6.6 %fusion.2 = f32[768,384]{1,0:T(8,128)S(1)} fusion(bf16[1536,4096]{1,0:T(8,128)(2,1)} %all-gather.4.cloned.1.call-done, s32[]{:T(128)S(6)} %select_n.35, bf16[1,4096,384]{2,1,0:T(8,128)(2,1)} %param.27), kind=kOutput, calls=%fused_computation.6 | convolution fusion | flops 2415919104 | bytes 10616836 | tf_op jit(solution)/shard_map/dot_general | solution.py:133
  168.4 0.7 copy-done.9
  169.2 0.9 copy-done.10
  170.1 3.5 %fusion.24 = bf16[768,384]{1,0:T(8,128)(2,1)S(1)} fusion(bf16[1,4096,384]{2,1,0:T(8,128)(2,1)S(1)} %copy-done.10, bf16[1536,4096]{1,0:T(8,128)(2,1)S(1)} %copy-done.9, s32[]{:T(128)S(6)} %select_n.35, f32[768,384]{1,0:T(8,128)S(1)} %fusion.2), kind=kOutput, calls=%fused_computation.20 | convolution fusion | flops 2417688576 | bytes 11206660 | tf_op jit(solution)/shard_map/dot_general | solution.py:134
  173.6 5.4 %convolution_convert_fusion = bf16[768,4096]{1,0:T(8,128)(2,1)} fusion(bf16[768,384]{1,0:T(8,128)(2,1)S(1)} %fusion.24, bf16[1,384,4096]{2,1,0:T(8,128)(2,1)S(1)} %copy-done), kind=kOutput, calls=%fused_computation.2 | convolution fusion | flops 2419064832 | bytes 10027008 | tf_op jit(solution)/shard_map/dot_general | solution.py:136
  179.0 0.2 collective-permute-start
  179.3 6.6 %fusion.6 = f32[768,384]{1,0:T(8,128)S(1)} fusion(bf16[1536,4096]{1,0:T(8,128)(2,1)} %all-gather.4.cloned.1.call-done, s32[]{:T(128)S(6)} %select_n.34, bf16[1,4096,384]{2,1,0:T(8,128)(2,1)} %param.27), kind=kOutput, calls=%fused_computation.10 | convolution fusion | flops 2415919104 | bytes 10616836 | tf_op jit(solution)/shard_map/dot_general | solution.py:133
  185.8 6.3 %fusion.29 = bf16[768,384]{1,0:T(8,128)(2,1)S(1)} fusion(bf16[1,4096,384]{2,1,0:T(8,128)(2,1)S(1)} %copy-done.11, bf16[1536,4096]{1,0:T(8,128)(2,1)} %all-gather.4.cloned.1.call-done, s32[]{:T(128)S(6)} %select_n.34, f32[768,384]{1,0:T(8,128)S(1)} %fusion.6), kind=kOutput, calls=%fused_computation.21 | convolution fusion | flops 2417688576 | bytes 11206660 | tf_op jit(solution)/shard_map/dot_general | solution.py:134
  192.1 7.2 %add_convert_fusion = bf16[768,4096]{1,0:T(8,128)(2,1)} fusion(bf16[768,4096]{1,0:T(8,128)(2,1)} %collective-permute-done, bf16[768,384]{1,0:T(8,128)(2,1)S(1)} %fusion.29, bf16[1,384,4096]{2,1,0:T(8,128)(2,1)S(1)} %copy-done), kind=kOutput, calls=%fused_computation | convolution fusion | flops 2431647744 | bytes 16318464 | tf_op jit(solution)/shard_map/dot_general | solution.py:136
  199.4 86.2 %reduce-scatter.2.cloned.1.call-done = bf16[48,4096]{1,0:T(8,128)(2,1)} async-done(((bf16[768,4096]{1,0:T(8,128)(2,1)}), bf16[48,4096]{1,0:T(8,128)(2,1)}) %reduce-scatter.2.cloned.1.call-update) | async-done | bytes 393232 | tf_op jit(solution)/shard_map/reduce_scatter | solution.py:143
  285.6 1.8 copy.57
  287.4 7.0 %all-to-all-start.1 = ((bf16[8,48,512]{2,1,0:T(8,128)(2,1)}), bf16[8,48,512]{2,1,0:T(8,128)(2,1)S(1)}, u32[]{:S(2)}, u32[]{:S(2)}) async-start(bf16[8,48,512]{2,1,0:T(8,128)(2,1)} %bitcast.77), calls=%async_computation.2 | async-start | bytes 786432 | tf_op jit(solution)/shard_map/all_to_all | solution.py:145
  294.4 0.7 select_reduce_fusion.1
  295.1 12.3 %all-to-all-done.1 = bf16[8,48,512]{2,1,0:T(8,128)(2,1)S(1)} async-done(((bf16[8,48,512]{2,1,0:T(8,128)(2,1)}), bf16[8,48,512]{2,1,0:T(8,128)(2,1)S(1)}, u32[]{:S(2)}, u32[]{:S(2)}) %all-to-all-start.1) | async-done | bytes 393248 | tf_op jit(solution)/shard_map/all_to_all | solution.py:145
  307.4 1.1 fusion.37
  (44 shorter events, 0.6 us)
Async XLA Ops:
  7.2 166.4 %copy-start = (bf16[1,384,4096]{2,1,0:T(8,128)(2,1)S(1)}, bf16[1,384,4096]{2,1,0:T(8,128)(2,1)}, u32[]{:S(2)}) copy-start(bf16[1,384,4096]{2,1,0:T(8,128)(2,1)} %param.29) | copy-start | bytes 9437188
  7.2 58.2 %all-gather.6.cloned.1.call-start = ((), (), s32[]{:S(2)}) async-start(), calls=%async_computation.5 | async-start | bytes 4392960 | tf_op jit(solution)/shard_map/all_gather | solution.py:49
  11.5 150.4 %all-gather.4.cloned.1.call-start = ((), (), s32[]{:S(2)}) async-start(), calls=%async_computation.3 | async-start | bytes 12976128 | tf_op jit(solution)/shard_map/all_gather | solution.py:127
  15.0 56.4 %copy-start.3 = (bf16[128,128]{1,0:T(8,128)(2,1)S(1)}, bf16[128,128]{1,0:T(8,128)(2,1)}, u32[]{:S(2)}) copy-start(bf16[128,128]{1,0:T(8,128)(2,1)} %param.21) | copy-start | bytes 98308
  66.7 5.0 %copy-start.6 = (pred[128,128]{1,0:T(8,128)(4,1)S(1)}, pred[128,128]{1,0:T(8,128)(4,1)}, u32[]{:S(2)}) copy-start(pred[128,128]{1,0:T(8,128)(4,1)} %iota_compare_fusion.1) | copy-start | bytes 49156
  66.9 4.8 %copy-start.2 = (f32[128,512]{0,1:T(8,128)S(1)}, f32[128,512]{0,1:T(8,128)}, u32[]{:S(2)}) copy-start(f32[128,512]{0,1:T(8,128)} %copy.48) | copy-start | bytes 786436
  66.9 4.8 %copy-start.4 = (f32[128,128]{1,0:T(8,128)S(1)}, f32[128,128]{1,0:T(8,128)}, u32[]{:S(2)}) copy-start(f32[128,128]{1,0:T(8,128)} %fusion.77) | copy-start | bytes 196612
  66.9 7.2 %copy-start.8 = (f32[512]{0:T(512)S(1)}, f32[512]{0:T(512)}, u32[]{:S(2)}) copy-start(f32[512]{0:T(512)} %param.24) | copy-start | bytes 6148
  73.3 25.1 %copy-start.5 = (f32[4096]{0:T(1024)S(1)}, f32[4096]{0:T(1024)}, u32[]{:S(2)}) copy-start(f32[4096]{0:T(1024)} %param.26) | copy-start | bytes 49156
  75.2 0.7 copy-start.1
  99.3 186.3 %reduce-scatter.2.cloned.1.call-start = ((), (), s32[]{:S(2)}) async-start(), calls=%async_computation.4 | async-start | bytes 6684672 | tf_op jit(solution)/shard_map/reduce_scatter | solution.py:143
  161.9 7.3 %copy-start.9 = (bf16[1536,4096]{1,0:T(8,128)(2,1)S(1)}, bf16[1536,4096]{1,0:T(8,128)(2,1)}, u32[]{:S(2)}) copy-start(bf16[1536,4096]{1,0:T(8,128)(2,1)} %all-gather.4.cloned.1.call-done) | copy-start | bytes 37748740
  161.9 8.2 %copy-start.10 = (bf16[1,4096,384]{2,1,0:T(8,128)(2,1)S(1)}, bf16[1,4096,384]{2,1,0:T(8,128)(2,1)}, u32[]{:S(2)}) copy-start(bf16[1,4096,384]{2,1,0:T(8,128)(2,1)} %param.28) | copy-start | bytes 9437188
  179.0 13.1 %collective-permute-start = (bf16[768,4096]{1,0:T(8,128)(2,1)}, bf16[768,4096]{1,0:T(8,128)(2,1)}, u32[]{:S(2)}, u32[]{:S(2)}) collective-permute-start(bf16[768,4096]{1,0:T(8,128)(2,1)} %convolution_convert_fusion), channel_id=1, source_target_pairs={{0,8},{8,0},{1,9},{9,1},{2,10},{10,2},{3,11},{11,3},{4,12},{12,4},... | collective-permute-start | bytes 18874376 | tf_op jit(solution)/shard_map/ppermute | solution.py:138
  179.2 6.6 %copy-start.11 = (bf16[1,4096,384]{2,1,0:T(8,128)(2,1)S(1)}, bf16[1,4096,384]{2,1,0:T(8,128)(2,1)}, u32[]{:S(2)}) copy-start(bf16[1,4096,384]{2,1,0:T(8,128)(2,1)} %param.28) | copy-start | bytes 9437188
  199.4 95.0 %copy-start.7 = (s32[128,2]{0,1:T(2,128)S(1)}, s32[128,2]{0,1:T(2,128)}, u32[]{:S(2)}) copy-start(s32[128,2]{0,1:T(2,128)} %param.30) | copy-start | bytes 3076
  287.4 20.0 %all-to-all-start.1 = ((bf16[8,48,512]{2,1,0:T(8,128)(2,1)}), bf16[8,48,512]{2,1,0:T(8,128)(2,1)S(1)}, u32[]{:S(2)}, u32[]{:S(2)}) async-start(bf16[8,48,512]{2,1,0:T(8,128)(2,1)} %bitcast.77), calls=%async_computation.2 | async-start | bytes 786432 | tf_op jit(solution)/shard_map/all_to_all | solution.py:145
Sparse Core Ops, SparseCore 0:
  11.6 53.7 all-gather.5
  99.4 62.4 all-gather.3
  199.5 86.0 reduce-scatter.1

commit v7 on v6

--- a/solution.py
+++ b/solution.py
@@ -124,22 +124,21 @@
     gate_here = gate_weight[0]
     up_here = up_weight[0]
     down_here = down_weight[0]
-    token_piece = lax.all_gather(chosen, ("core", "chip"), axis=0, tiled=True)
-    core = lax.axis_index("core")
-    half = token_piece.shape[0] // lax.axis_size("core")
+    swap = [(0, 1), (1, 0)]
+    gate_other = lax.ppermute(gate_here, "core", swap)
+    up_other = lax.ppermute(up_here, "core", swap)
+    down_other = lax.ppermute(down_here, "core", swap)
+    token_piece = lax.all_gather(chosen, "chip", axis=0, tiled=True)
 
-    def expert_rows(which):
-        rows = lax.dynamic_slice_in_dim(token_piece, which * half, half, 0)
-        gate_proj = jnp.dot(rows, gate_here, preferred_element_type=jnp.float32)
-        up_proj = jnp.dot(rows, up_here, preferred_element_type=jnp.float32)
+    def through(gate_part, up_part, down_part):
+        gate_proj = jnp.dot(token_piece, gate_part, preferred_element_type=jnp.float32)
+        up_proj = jnp.dot(token_piece, up_part, preferred_element_type=jnp.float32)
         hidden = (jax.nn.silu(gate_proj) * up_proj).astype(jnp.bfloat16)
-        return jnp.dot(hidden, down_here, preferred_element_type=jnp.float32)
+        return jnp.dot(hidden, down_part, preferred_element_type=jnp.float32).astype(jnp.bfloat16)
 
-    moved = lax.ppermute(expert_rows(1 - core).astype(jnp.bfloat16), "core", [(0, 1), (1, 0)])
-    own_part = expert_rows(core)
-    pair_sum = (own_part.astype(jnp.bfloat16).astype(jnp.float32) + moved.astype(jnp.float32)).astype(
-        jnp.bfloat16
-    )
+    own_part = through(gate_here, up_here, down_here)
+    other_part = through(gate_other, up_other, down_other)
+    pair_sum = (own_part.astype(jnp.float32) + other_part.astype(jnp.float32)).astype(jnp.bfloat16)
     summed = lax.psum_scatter(pair_sum, "chip", scatter_dimension=0, tiled=True)
     outgoing = jnp.transpose(summed.reshape(capacity, exp_count, channels), (1, 0, 2))
     returned = lax.all_to_all(outgoing, "exp", 0, 0)

time: 316 us -> 311 us (0.984)
  local copies, waits for them, and re-layouts: 9.2 us -> 4.92 us
    dot_general x6 -> x4, matrix products: 35.6 us -> 38.5 us  [the longest x2 25.3 us: through(): jnp.dot(hidden, down_part, preferred_element_type=jnp.float32)]
  transfers between devices with their start and end apart: 5 -> 7, of which waited for: 4 -> 4; matrix products, arithmetic and copies ran while one was open for 6% -> 9% of each run, Pallas kernels for 0% -> 0%
where the time goes in v7:
time: 311 us; the launch traced here: 310 us
  waiting for transfers between devices  210 us (68%)
  matrix products  42 us (14%)
  blocking collectives  22 us (7%)
  between operations  14.1 us (5%)
  other arithmetic  9.54 us (3%)
  starting transfers between devices  7.8 us (3%)
  local copies, waits for them, and re-layouts  4.92 us (2%)
    reduce_scatter x1, waiting for transfers between devices, on_device(): summed = lax.psum_scatter(pair_sum, 'chip', scatter_dimension=0, tiled=True)  86.1 us
    all_gather x1, waiting for transfers between devices, on_device(): token_piece = lax.all_gather(chosen, 'chip', axis=0, tiled=True)  60.3 us
    all_gather x1, waiting for transfers between devices, carried_state(): everything = lax.all_gather(packed, CTX)  50.7 us
    dot_general x2, matrix products, through(): jnp.dot(hidden, down_part, preferred_element_type=jnp.float32)  25.3 us
    all_to_all x1, blocking collectives, on_device(): arrived = lax.all_to_all(picked, 'exp', 0, 0)  22 us
    dot_general x2, matrix products, through(): jnp.dot(token_piece, gate_part, preferred_element_type=jnp.float32)  13.2 us
    all_to_all x1, waiting for transfers between devices, on_device(): returned = lax.all_to_all(outgoing, 'exp', 0, 0)  13 us
    all_to_all x1, starting transfers between devices, on_device(): returned = lax.all_to_all(outgoing, 'exp', 0, 0)  6.99 us
  transfers between devices with their start and end apart: 7, of which 4 were waited for; matrix products, arithmetic and copies ran while one was open for 9% of the time, Pallas kernels for 0%

profile of v7, /device:TPU:2, one launch (start us, length us, event | category | flops | bytes accessed | tf_op | source)
XLA Modules:
  0.0 310.5 jit_solution(16454368562569605135)
XLA Ops:
  7.2 0.0 all-gather.6.cloned.1.call-start
  7.2 0.8 negate_multiply_fusion
  8.0 0.1 copy.40
  8.1 0.2 reduce_window_sum.22
  8.4 1.0 copy.43
  9.4 0.3 convolution_convert_fusion.3
  9.7 0.2 scatter.9
  9.9 0.7 pad_maximum_fusion
  10.5 0.0 all-gather.6.cloned.1.call-update
  10.5 0.0 all-gather.4.cloned.1.call-start
  10.7 0.1 copy.44
  10.7 1.0 convert_multiply_fusion.1
  11.7 0.1 copy.48
  11.9 0.7 fusion.37
  12.6 0.3 reduce_window_sum.23
  12.9 0.9 fusion.51
  13.8 50.7 %all-gather.6.cloned.1.call-done = bf16[16640,128]{1,0:T(8,128)(2,1)} async-done(((bf16[520,128]{1,0:T(8,128)(2,1)}), bf16[16640,128]{1,0:T(8,128)(2,1)}) %all-gather.6.cloned.1.call-update) | async-done | bytes 4259856 | tf_op jit(solution)/shard_map/all_gather | solution.py:49
  64.4 0.9 fusion.47
  65.4 0.1 copy.52
  65.5 0.1 copy.53
  65.6 0.1 select_reduce_fusion
  65.7 0.1 exponential_select_fusion
  65.7 0.1 mul.95
  65.8 0.1 mul.96
  66.0 4.5 %multiply_reduce_fusion = f32[512,128]{1,0:T(8,128)S(1)} fusion(bf16[32,520,128]{2,1,0:T(8,128)(2,1)} %bitcast.67, f32[32,512]{1,0:T(8,128)S(1)} %mul.96), kind=kLoop, calls=%fused_computation.1 | loop fusion | flops 6225920 | bytes 4521984 | tf_op jit(solution)/shard_map/reduce_sum | solution.py:63
  70.4 0.3 fusion.3
  70.7 0.8 multiply_reduce_fusion.1
  71.6 0.1 copy.49
  71.8 0.2 convolution_convert_fusion.2
  72.0 22.0 %all_to_all.10 = bf16[8,48,512]{2,1,0:T(8,128)(2,1)S(1)} all-to-all(bf16[8,48,512]{2,1,0:T(8,128)(2,1)S(1)} %convolution_convert_fusion.2), channel_id=1, replica_groups=mesh['chip'=16,'core'=2,'exp'=8] {'exp'}, dimensions={0} | all-to-all | bytes 786432 | tf_op jit(solution)/shard_map/all_to_all | solution.py:115
  94.1 0.1 convert_bitcast_fusion
  94.2 0.1 copy.55
  94.2 0.2 fusion.5
  94.4 0.9 multiply_convert_fusion.1
  95.3 0.0 reduce-scatter.2.cloned.1.call-start
  95.4 0.1 collective-permute-start
  95.5 0.5 collective-permute-start.1
  96.0 0.1 collective-permute-start.2
  96.1 60.3 %all-gather.4.cloned.1.call-done = bf16[768,4096]{1,0:T(8,128)(2,1)} async-done(((bf16[48,4096]{1,0:T(8,128)(2,1)}), bf16[768,4096]{1,0:T(8,128)(2,1)}) %all-gather.4.cloned.1.call-update) | async-done | bytes 6291472 | tf_op jit(solution)/shard_map/all_gather | solution.py:131
  156.4 6.7 %fusion.41 = f32[768,384]{1,0:T(8,128)} fusion(bf16[768,4096]{1,0:T(8,128)(2,1)} %all-gather.4.cloned.1.call-done, bf16[1,4096,384]{2,1,0:T(8,128)(2,1)S(1)} %copy-done.9), kind=kOutput, calls=%fused_computation.79 | convolution fusion | flops 2415919104 | bytes 10616832 | tf_op jit(solution)/shard_map/dot_general | solution.py:134
  163.1 6.5 %fusion.52 = f32[768,384]{1,0:T(8,128)} fusion(bf16[768,4096]{1,0:T(8,128)(2,1)S(1)} %copy-done.8, bf16[4096,384]{1,0:T(8,128)(2,1)} %collective-permute-done), kind=kOutput, calls=%fused_computation.89 | convolution fusion | flops 2415919104 | bytes 10616832 | tf_op jit(solution)/shard_map/dot_general | solution.py:134
  169.6 11.7 %convolution_convert_fusion.1 = bf16[768,4096]{1,0:T(8,128)(2,1)} fusion(bf16[768,4096]{1,0:T(8,128)(2,1)} %all-gather.4.cloned.1.call-done, f32[768,384]{1,0:T(8,128)} %fusion.41, bf16[1,384,4096]{2,1,0:T(8,128)(2,1)} %param.29, bf16[1,4096,384]{2,1,0:T(8,128)(2,1)S(1)} %copy-done.10), kind=kOutput, calls=%fused_computation.3 | convolution fusion | flops 4836753408 | bytes 20054016 | tf_op jit(solution)/shard_map/dot_general | solution.py:137
  181.3 13.6 %add_convert_fusion = bf16[768,4096]{1,0:T(8,128)(2,1)} fusion(bf16[768,4096]{1,0:T(8,128)(2,1)} %convolution_convert_fusion.1, bf16[384,4096]{1,0:T(8,128)(2,1)} %collective-permute-done.2, f32[768,384]{1,0:T(8,128)} %fusion.52, bf16[768,4096]{1,0:T(8,128)(2,1)} %all-gather.4.cloned.1.call-done, bf16[4096,384]{1,0:T(8,128)(2,1)} %collective-permute-done.1), kind=kOutput, calls=%fused_computation | convolution fusion | flops 4849336320 | bytes 26345472 | tf_op jit(solution)/shard_map/dot_general | solution.py:137
  194.9 86.1 %reduce-scatter.2.cloned.1.call-done = bf16[48,4096]{1,0:T(8,128)(2,1)} async-done(((bf16[768,4096]{1,0:T(8,128)(2,1)}), bf16[48,4096]{1,0:T(8,128)(2,1)}) %reduce-scatter.2.cloned.1.call-update) | async-done | bytes 393232 | tf_op jit(solution)/shard_map/reduce_scatter | solution.py:142
  281.1 1.8 copy.57
  282.8 7.0 %all-to-all-start.1 = ((bf16[8,48,512]{2,1,0:T(8,128)(2,1)}), bf16[8,48,512]{2,1,0:T(8,128)(2,1)S(1)}, u32[]{:S(2)}, u32[]{:S(2)}) async-start(bf16[8,48,512]{2,1,0:T(8,128)(2,1)} %bitcast.65), calls=%async_computation.2 | async-start | bytes 786432 | tf_op jit(solution)/shard_map/all_to_all | solution.py:144
  289.9 13.0 %all-to-all-done.1 = bf16[8,48,512]{2,1,0:T(8,128)(2,1)S(1)} async-done(((bf16[8,48,512]{2,1,0:T(8,128)(2,1)}), bf16[8,48,512]{2,1,0:T(8,128)(2,1)S(1)}, u32[]{:S(2)}, u32[]{:S(2)}) %all-to-all-start.1) | async-done | bytes 393248 | tf_op jit(solution)/shard_map/all_to_all | solution.py:144
  302.8 1.1 fusion.4
  (44 shorter events, 0.4 us)
Async XLA Ops:
  7.2 2.3 copy-start
  7.2 57.3 %all-gather.6.cloned.1.call-start = ((), (), s32[]{:S(2)}) async-start(), calls=%async_computation.5 | async-start | bytes 4392960 | tf_op jit(solution)/shard_map/all_gather | solution.py:49
  10.5 145.8 %all-gather.4.cloned.1.call-start = ((), (), s32[]{:S(2)}) async-start(), calls=%async_computation.3 | async-start | bytes 6684672 | tf_op jit(solution)/shard_map/all_gather | solution.py:131
  10.6 59.8 %copy-start.2 = (bf16[128,128]{1,0:T(8,128)(2,1)S(1)}, bf16[128,128]{1,0:T(8,128)(2,1)}, u32[]{:S(2)}) copy-start(bf16[128,128]{1,0:T(8,128)(2,1)} %param.21) | copy-start | bytes 98308
  65.9 5.8 %copy-start.3 = (bf16[128,512]{1,0:T(8,128)(2,1)S(1)}, bf16[128,512]{1,0:T(8,128)(2,1)}, u32[]{:S(2)}) copy-start(bf16[128,512]{1,0:T(8,128)(2,1)} %param.25) | copy-start | bytes 393220
  66.0 5.8 %copy-start.6 = (f32[512]{0:T(512)S(1)}, f32[512]{0:T(512)}, u32[]{:S(2)}) copy-start(f32[512]{0:T(512)} %param.24) | copy-start | bytes 6148
  71.5 22.9 %copy-start.4 = (f32[4096]{0:T(1024)S(1)}, f32[4096]{0:T(1024)}, u32[]{:S(2)}) copy-start(f32[4096]{0:T(1024)} %param.26) | copy-start | bytes 49156
  71.8 91.3 %copy-start.1 = (bf16[128,512]{1,0:T(8,128)(2,1)}, bf16[128,512]{1,0:T(8,128)(2,1)S(1)}, u32[]{:S(2)}) copy-start(bf16[128,512]{1,0:T(8,128)(2,1)S(1)} %add_convert_fusion.1) | copy-start | bytes 393220
  71.8 23.6 %copy-start.9 = (bf16[1,4096,384]{2,1,0:T(8,128)(2,1)S(1)}, bf16[1,4096,384]{2,1,0:T(8,128)(2,1)}, u32[]{:S(2)}) copy-start(bf16[1,4096,384]{2,1,0:T(8,128)(2,1)} %param.27) | copy-start | bytes 9437188
  95.3 185.7 %reduce-scatter.2.cloned.1.call-start = ((), (), s32[]{:S(2)}) async-start(), calls=%async_computation.4 | async-start | bytes 6684672 | tf_op jit(solution)/shard_map/reduce_scatter | solution.py:142
  95.4 67.7 %collective-permute-start = (bf16[4096,384]{1,0:T(8,128)(2,1)S(1)}, bf16[4096,384]{1,0:T(8,128)(2,1)}, u32[]{:S(2)}, u32[]{:S(2)}) collective-permute-start(bf16[4096,384]{1,0:T(8,128)(2,1)S(1)} %bitcast.76), channel_id=1, source_target_pairs={{0,8},{8,0},{1,9},{9,1},{2,10},{10,2},{3,11},{11,3},{4,12},{12,4},... | collective-permute-start | bytes 9437192 | tf_op jit(solution)/shard_map/ppermute | solution.py:128
  95.5 85.8 %collective-permute-start.1 = (bf16[4096,384]{1,0:T(8,128)(2,1)}, bf16[4096,384]{1,0:T(8,128)(2,1)}, u32[]{:S(2)}, u32[]{:S(2)}) collective-permute-start(bf16[4096,384]{1,0:T(8,128)(2,1)} %bitcast.77), channel_id=1, source_target_pairs={{0,8},{8,0},{1,9},{9,1},{2,10},{10,2},{3,11},{11,3},{4,12},{12,4},... | collective-permute-start | bytes 9437192 | tf_op jit(solution)/shard_map/ppermute | solution.py:129
  96.0 85.3 %collective-permute-start.2 = (bf16[384,4096]{1,0:T(8,128)(2,1)}, bf16[384,4096]{1,0:T(8,128)(2,1)}, u32[]{:S(2)}, u32[]{:S(2)}) collective-permute-start(bf16[384,4096]{1,0:T(8,128)(2,1)} %bitcast.78), channel_id=1, source_target_pairs={{0,8},{8,0},{1,9},{9,1},{2,10},{10,2},{3,11},{11,3},{4,12},{12,4},... | collective-permute-start | bytes 9437192 | tf_op jit(solution)/shard_map/ppermute | solution.py:130
  156.4 6.7 %copy-start.8 = (bf16[768,4096]{1,0:T(8,128)(2,1)S(1)}, bf16[768,4096]{1,0:T(8,128)(2,1)}, u32[]{:S(2)}) copy-start(bf16[768,4096]{1,0:T(8,128)(2,1)} %all-gather.4.cloned.1.call-done) | copy-start | bytes 18874372
  163.1 6.5 %copy-start.10 = (bf16[1,4096,384]{2,1,0:T(8,128)(2,1)S(1)}, bf16[1,4096,384]{2,1,0:T(8,128)(2,1)}, u32[]{:S(2)}) copy-start(bf16[1,4096,384]{2,1,0:T(8,128)(2,1)} %param.28) | copy-start | bytes 9437188
  194.9 94.9 %copy-start.5 = (s32[128,2]{0,1:T(2,128)S(1)}, s32[128,2]{0,1:T(2,128)}, u32[]{:S(2)}) copy-start(s32[128,2]{0,1:T(2,128)} %param.30) | copy-start | bytes 3076
  194.9 94.9 %copy-start.7 = (f32[128,2]{0,1:T(2,128)S(1)}, f32[128,2]{0,1:T(2,128)}, u32[]{:S(2)}) copy-start(f32[128,2]{0,1:T(2,128)} %param.31) | copy-start | bytes 3076
  282.8 20.0 %all-to-all-start.1 = ((bf16[8,48,512]{2,1,0:T(8,128)(2,1)}), bf16[8,48,512]{2,1,0:T(8,128)(2,1)S(1)}, u32[]{:S(2)}, u32[]{:S(2)}) async-start(bf16[8,48,512]{2,1,0:T(8,128)(2,1)} %bitcast.65), calls=%async_computation.2 | async-start | bytes 786432 | tf_op jit(solution)/shard_map/all_to_all | solution.py:144
Sparse Core Ops, SparseCore 0:
  10.7 53.7 all-gather.5
  95.5 60.8 all-gather.3
  195.1 85.9 reduce-scatter.1

commit v8 on v7

--- a/solution.py
+++ b/solution.py
@@ -130,15 +130,13 @@
     down_other = lax.ppermute(down_here, "core", swap)
     token_piece = lax.all_gather(chosen, "chip", axis=0, tiled=True)
 
-    def through(gate_part, up_part, down_part):
-        gate_proj = jnp.dot(token_piece, gate_part, preferred_element_type=jnp.float32)
-        up_proj = jnp.dot(token_piece, up_part, preferred_element_type=jnp.float32)
-        hidden = (jax.nn.silu(gate_proj) * up_proj).astype(jnp.bfloat16)
-        return jnp.dot(hidden, down_part, preferred_element_type=jnp.float32).astype(jnp.bfloat16)
-
-    own_part = through(gate_here, up_here, down_here)
-    other_part = through(gate_other, up_other, down_other)
-    pair_sum = (own_part.astype(jnp.float32) + other_part.astype(jnp.float32)).astype(jnp.bfloat16)
+    gate_both = jnp.concatenate([gate_here, gate_other], axis=1)
+    up_both = jnp.concatenate([up_here, up_other], axis=1)
+    down_both = jnp.concatenate([down_here, down_other], axis=0)
+    gate_proj = jnp.dot(token_piece, gate_both, preferred_element_type=jnp.float32)
+    up_proj = jnp.dot(token_piece, up_both, preferred_element_type=jnp.float32)
+    hidden = (jax.nn.silu(gate_proj) * up_proj).astype(jnp.bfloat16)
+    pair_sum = jnp.dot(hidden, down_both, preferred_element_type=jnp.float32).astype(jnp.bfloat16)
     summed = lax.psum_scatter(pair_sum, "chip", scatter_dimension=0, tiled=True)
     outgoing = jnp.transpose(summed.reshape(capacity, exp_count, channels), (1, 0, 2))
     returned = lax.all_to_all(outgoing, "exp", 0, 0)

time: 311 us -> 298 us (0.958)
  matrix products: 42 us -> 29.3 us
    dot_general x4 -> x3, matrix products: 38.5 us -> 25.7 us  [the longest x1 9.77 us: on_device(): jnp.dot(token_piece, gate_both, preferred_element_type=jnp.float32)]
    ppermute x1, waiting for transfers between devices: 0.01 us -> 5.38 us  [on_device(): gate_other = lax.ppermute(gate_here, 'core', swap)]
    all_gather x1, waiting for transfers between devices: 60.3 us -> 54.9 us  [on_device(): token_piece = lax.all_gather(chosen, 'chip', axis=0, tiled=True)]
  transfers between devices with their start and end apart: 7 -> 7, of which waited for: 4 -> 5; matrix products, arithmetic and copies ran while one was open for 9% -> 7% of each run, Pallas kernels for 0% -> 0%
where the time goes in v8:
time: 298 us
  waiting for transfers between devices  210 us (70%)
  matrix products  29.3 us (10%)
  blocking collectives  21.9 us (7%)
  between operations  14.1 us (5%)
  other arithmetic  9.51 us (3%)
  starting transfers between devices  7.8 us (3%)
  local copies, waits for them, and re-layouts  4.92 us (2%)
    reduce_scatter x1, waiting for transfers between devices, on_device(): summed = lax.psum_scatter(pair_sum, 'chip', scatter_dimension=0, tiled=True)  86.4 us
    all_gather x1, waiting for transfers between devices, on_device(): token_piece = lax.all_gather(chosen, 'chip', axis=0, tiled=True)  54.9 us
    all_gather x1, waiting for transfers between devices, carried_state(): everything = lax.all_gather(packed, CTX)  50.6 us
    all_to_all x1, blocking collectives, on_device(): arrived = lax.all_to_all(picked, 'exp', 0, 0)  21.9 us
    all_to_all x1, waiting for transfers between devices, on_device(): returned = lax.all_to_all(outgoing, 'exp', 0, 0)  13.1 us
    dot_general x1, matrix products, on_device(): jnp.dot(token_piece, gate_both, preferred_element_type=jnp.float32)  9.77 us
    dot_general x1, matrix products, on_device(): jnp.dot(hidden, down_both, preferred_element_type=jnp.float32)  8.86 us
    dot_general x1, matrix products, on_device(): up_proj = jnp.dot(token_piece, up_both, preferred_element_type=jnp.float32)  7.1 us
  transfers between devices with their start and end apart: 7, of which 5 were waited for; matrix products, arithmetic and copies ran while one was open for 7% of the time, Pallas kernels for 0%

profile of v8, /device:TPU:2, one launch (start us, length us, event | category | flops | bytes accessed | tf_op | source)
XLA Modules:
  0.0 297.9 jit_solution(14104984194117521374)
XLA Ops:
  7.2 0.0 all-gather.6.cloned.1.call-start
  7.2 0.8 negate_multiply_fusion
  8.0 0.1 copy.40
  8.1 0.2 reduce_window_sum.22
  8.4 1.0 copy.43
  9.4 0.3 convolution_convert_fusion.2
  9.7 0.2 scatter.9
  9.9 0.7 pad_maximum_fusion
  10.5 0.0 all-gather.6.cloned.1.call-update
  10.6 0.0 all-gather.4.cloned.1.call-start
  10.7 0.1 copy.44
  10.7 1.0 convert_multiply_fusion.1
  11.8 0.1 copy.48
  11.9 0.7 fusion.46
  12.6 0.3 reduce_window_sum.23
  12.9 0.9 fusion.55
  13.8 50.6 %all-gather.6.cloned.1.call-done = bf16[16640,128]{1,0:T(8,128)(2,1)} async-done(((bf16[520,128]{1,0:T(8,128)(2,1)}), bf16[16640,128]{1,0:T(8,128)(2,1)}) %all-gather.6.cloned.1.call-update) | async-done | bytes 4259856 | tf_op jit(solution)/shard_map/all_gather | solution.py:49
  64.4 0.9 fusion.53
  65.4 0.1 copy.52
  65.5 0.1 copy.53
  65.6 0.1 select_reduce_fusion
  65.7 0.1 exponential_select_fusion
  65.8 0.1 mul.89
  65.9 0.1 mul.90
  66.0 4.4 %multiply_reduce_fusion = f32[512,128]{1,0:T(8,128)S(1)} fusion(bf16[32,520,128]{2,1,0:T(8,128)(2,1)} %bitcast.55, f32[32,512]{1,0:T(8,128)S(1)} %mul.90), kind=kLoop, calls=%fused_computation | loop fusion | flops 6225920 | bytes 4521984 | tf_op jit(solution)/shard_map/reduce_sum | solution.py:63
  70.4 0.3 fusion.14
  70.7 0.8 multiply_reduce_fusion.1
  71.5 0.1 copy.49
  71.7 0.2 convolution_convert_fusion.1
  72.0 21.9 %all_to_all.10 = bf16[8,48,512]{2,1,0:T(8,128)(2,1)S(1)} all-to-all(bf16[8,48,512]{2,1,0:T(8,128)(2,1)S(1)} %convolution_convert_fusion.1), channel_id=1, replica_groups=mesh['chip'=16,'core'=2,'exp'=8] {'exp'}, dimensions={0} | all-to-all | bytes 786432 | tf_op jit(solution)/shard_map/all_to_all | solution.py:115
  93.9 0.1 convert_bitcast_fusion
  94.0 0.1 copy.55
  94.0 0.2 fusion.16
  94.2 0.9 multiply_convert_fusion.2
  95.2 0.0 reduce-scatter.2.cloned.1.call-start
  95.2 0.1 collective-permute-start
  95.3 0.5 collective-permute-start.1
  95.8 0.1 collective-permute-start.2
  95.9 5.4 %collective-permute-done = bf16[4096,384]{1,0:T(8,128)(2,1)} collective-permute-done((bf16[4096,384]{1,0:T(8,128)(2,1)}, bf16[4096,384]{1,0:T(8,128)(2,1)}, u32[]{:S(2)}, u32[]{:S(2)}) %collective-permute-start) | collective-permute-done | bytes 3145760 | tf_op jit(solution)/shard_map/ppermute | solution.py:128
  101.3 54.9 %all-gather.4.cloned.1.call-done = bf16[768,4096]{1,0:T(8,128)(2,1)} async-done(((bf16[48,4096]{1,0:T(8,128)(2,1)}), bf16[768,4096]{1,0:T(8,128)(2,1)}) %all-gather.4.cloned.1.call-update) | async-done | bytes 6291472 | tf_op jit(solution)/shard_map/all_gather | solution.py:131
  156.2 9.8 %fusion = f32[768,768]{1,0:T(8,128)S(1)} fusion(bf16[768,4096]{1,0:T(8,128)(2,1)} %all-gather.4.cloned.1.call-done, bf16[4096,384]{1,0:T(8,128)(2,1)} %collective-permute-done, bf16[4096,384]{1,0:T(8,128)(2,1)} %bitcast.65), kind=kOutput, calls=%fused_computation.2 | convolution fusion | flops 4844421120 | bytes 14942208 | tf_op jit(solution)/shard_map/dot_general | solution.py:136
  166.0 7.1 %fusion.4 = f32[768,768]{1,0:T(8,128)S(1)} fusion(bf16[768,4096]{1,0:T(8,128)(2,1)S(1)} %copy-done.8, bf16[4096,384]{1,0:T(8,128)(2,1)} %collective-permute-done.1, bf16[4096,384]{1,0:T(8,128)(2,1)S(1)} %bitcast.67), kind=kOutput, calls=%fused_computation.6 | convolution fusion | flops 4844421120 | bytes 14942208 | tf_op jit(solution)/shard_map/dot_general | solution.py:137
  173.1 8.9 %convolution_convert_fusion = bf16[768,4096]{1,0:T(8,128)(2,1)} fusion(bf16[384,4096]{1,0:T(8,128)(2,1)} %collective-permute-done.2, bf16[384,4096]{1,0:T(8,128)(2,1)S(1)} %bitcast.69, f32[768,768]{1,0:T(8,128)S(1)} %fusion.4, f32[768,768]{1,0:T(8,128)S(1)} %fusion), kind=kOutput, calls=%fused_computation.1 | convolution fusion | flops 4851105792 | bytes 17301504 | tf_op jit(solution)/shard_map/dot_general | solution.py:139
  182.0 86.4 %reduce-scatter.2.cloned.1.call-done = bf16[48,4096]{1,0:T(8,128)(2,1)} async-done(((bf16[768,4096]{1,0:T(8,128)(2,1)}), bf16[48,4096]{1,0:T(8,128)(2,1)}) %reduce-scatter.2.cloned.1.call-update) | async-done | bytes 393232 | tf_op jit(solution)/shard_map/reduce_scatter | solution.py:140
  268.4 1.8 copy.57
  270.2 7.0 %all-to-all-start.1 = ((bf16[8,48,512]{2,1,0:T(8,128)(2,1)}), bf16[8,48,512]{2,1,0:T(8,128)(2,1)S(1)}, u32[]{:S(2)}, u32[]{:S(2)}) async-start(bf16[8,48,512]{2,1,0:T(8,128)(2,1)} %bitcast.53), calls=%async_computation.2 | async-start | bytes 786432 | tf_op jit(solution)/shard_map/all_to_all | solution.py:142
  277.2 13.1 %all-to-all-done.1 = bf16[8,48,512]{2,1,0:T(8,128)(2,1)S(1)} async-done(((bf16[8,48,512]{2,1,0:T(8,128)(2,1)}), bf16[8,48,512]{2,1,0:T(8,128)(2,1)S(1)}, u32[]{:S(2)}, u32[]{:S(2)}) %all-to-all-start.1) | async-done | bytes 393248 | tf_op jit(solution)/shard_map/all_to_all | solution.py:142
  290.3 1.1 fusion.15
  (43 shorter events, 0.4 us)
Async XLA Ops:
  7.2 2.3 copy-start
  7.2 63.2 %copy-start.2 = (bf16[128,128]{1,0:T(8,128)(2,1)S(1)}, bf16[128,128]{1,0:T(8,128)(2,1)}, u32[]{:S(2)}) copy-start(bf16[128,128]{1,0:T(8,128)(2,1)} %param.21) | copy-start | bytes 98308
  7.2 57.3 %all-gather.6.cloned.1.call-start = ((), (), s32[]{:S(2)}) async-start(), calls=%async_computation.5 | async-start | bytes 4392960 | tf_op jit(solution)/shard_map/all_gather | solution.py:49
  10.6 145.6 %all-gather.4.cloned.1.call-start = ((), (), s32[]{:S(2)}) async-start(), calls=%async_computation.3 | async-start | bytes 6684672 | tf_op jit(solution)/shard_map/all_gather | solution.py:131
  11.7 59.9 %copy-start.3 = (bf16[128,512]{1,0:T(8,128)(2,1)S(1)}, bf16[128,512]{1,0:T(8,128)(2,1)}, u32[]{:S(2)}) copy-start(bf16[128,512]{1,0:T(8,128)(2,1)} %param.25) | copy-start | bytes 393220
  11.7 59.9 %copy-start.6 = (f32[512]{0:T(512)S(1)}, f32[512]{0:T(512)}, u32[]{:S(2)}) copy-start(f32[512]{0:T(512)} %param.24) | copy-start | bytes 6148
  70.4 23.9 %copy-start.4 = (f32[4096]{0:T(1024)S(1)}, f32[4096]{0:T(1024)}, u32[]{:S(2)}) copy-start(f32[4096]{0:T(1024)} %param.26) | copy-start | bytes 49156
  71.7 94.2 %copy-start.1 = (bf16[128,512]{1,0:T(8,128)(2,1)}, bf16[128,512]{1,0:T(8,128)(2,1)S(1)}, u32[]{:S(2)}) copy-start(bf16[128,512]{1,0:T(8,128)(2,1)S(1)} %add_convert_fusion) | copy-start | bytes 393220
  95.2 173.2 %reduce-scatter.2.cloned.1.call-start = ((), (), s32[]{:S(2)}) async-start(), calls=%async_computation.4 | async-start | bytes 6684672 | tf_op jit(solution)/shard_map/reduce_scatter | solution.py:140
  95.2 6.1 %collective-permute-start = (bf16[4096,384]{1,0:T(8,128)(2,1)}, bf16[4096,384]{1,0:T(8,128)(2,1)}, u32[]{:S(2)}, u32[]{:S(2)}) collective-permute-start(bf16[4096,384]{1,0:T(8,128)(2,1)} %bitcast.64), channel_id=1, source_target_pairs={{0,8},{8,0},{1,9},{9,1},{2,10},{10,2},{3,11},{11,3},{4,12},{12,4},... | collective-permute-start | bytes 9437192 | tf_op jit(solution)/shard_map/ppermute | solution.py:128
  95.3 70.7 %collective-permute-start.1 = (bf16[4096,384]{1,0:T(8,128)(2,1)}, bf16[4096,384]{1,0:T(8,128)(2,1)}, u32[]{:S(2)}, u32[]{:S(2)}) collective-permute-start(bf16[4096,384]{1,0:T(8,128)(2,1)} %bitcast.66), channel_id=1, source_target_pairs={{0,8},{8,0},{1,9},{9,1},{2,10},{10,2},{3,11},{11,3},{4,12},{12,4},... | collective-permute-start | bytes 9437192 | tf_op jit(solution)/shard_map/ppermute | solution.py:129
  95.8 70.2 %copy-start.9 = (bf16[1,4096,384]{2,1,0:T(8,128)(2,1)S(1)}, bf16[1,4096,384]{2,1,0:T(8,128)(2,1)}, u32[]{:S(2)}) copy-start(bf16[1,4096,384]{2,1,0:T(8,128)(2,1)} %param.28) | copy-start | bytes 9437188
  95.8 77.3 %collective-permute-start.2 = (bf16[384,4096]{1,0:T(8,128)(2,1)}, bf16[384,4096]{1,0:T(8,128)(2,1)}, u32[]{:S(2)}, u32[]{:S(2)}) collective-permute-start(bf16[384,4096]{1,0:T(8,128)(2,1)} %bitcast.68), channel_id=1, source_target_pairs={{0,8},{8,0},{1,9},{9,1},{2,10},{10,2},{3,11},{11,3},{4,12},{12,4},... | collective-permute-start | bytes 9437192 | tf_op jit(solution)/shard_map/ppermute | solution.py:130
  156.2 9.8 %copy-start.8 = (bf16[768,4096]{1,0:T(8,128)(2,1)S(1)}, bf16[768,4096]{1,0:T(8,128)(2,1)}, u32[]{:S(2)}) copy-start(bf16[768,4096]{1,0:T(8,128)(2,1)} %all-gather.4.cloned.1.call-done) | copy-start | bytes 18874372
  166.0 7.2 %copy-start.10 = (bf16[1,384,4096]{2,1,0:T(8,128)(2,1)S(1)}, bf16[1,384,4096]{2,1,0:T(8,128)(2,1)}, u32[]{:S(2)}) copy-start(bf16[1,384,4096]{2,1,0:T(8,128)(2,1)} %param.29) | copy-start | bytes 9437188
  182.0 95.2 %copy-start.5 = (s32[128,2]{0,1:T(2,128)S(1)}, s32[128,2]{0,1:T(2,128)}, u32[]{:S(2)}) copy-start(s32[128,2]{0,1:T(2,128)} %param.30) | copy-start | bytes 3076
  182.0 95.2 %copy-start.7 = (f32[128,2]{0,1:T(2,128)S(1)}, f32[128,2]{0,1:T(2,128)}, u32[]{:S(2)}) copy-start(f32[128,2]{0,1:T(2,128)} %param.31) | copy-start | bytes 3076
  270.2 20.1 %all-to-all-start.1 = ((bf16[8,48,512]{2,1,0:T(8,128)(2,1)}), bf16[8,48,512]{2,1,0:T(8,128)(2,1)S(1)}, u32[]{:S(2)}, u32[]{:S(2)}) async-start(bf16[8,48,512]{2,1,0:T(8,128)(2,1)} %bitcast.53), calls=%async_computation.2 | async-start | bytes 786432 | tf_op jit(solution)/shard_map/all_to_all | solution.py:142
Sparse Core Ops, SparseCore 0:
  10.7 53.7 all-gather.5
  95.3 60.8 all-gather.3
  182.2 86.1 reduce-scatter.1

commit v9 on v8

--- a/solution.py
+++ b/solution.py
@@ -57,10 +57,11 @@
     between = (shard_of[:, None] < shard_of[None, :]) & (shard_of[None, :] < me)
     spans = jnp.sum(jnp.where(between[:, :, None], decay_all[None, :, :], 0.0), axis=1)
     weight = jnp.where((shard_of < me)[:, None], jnp.exp(spans), 0.0)
-    gathered = everything[:, :rows, :].astype(jnp.float32).reshape(
-        shards, head_count, head_width, nstate
+    gathered = everything[:, :rows, :].reshape(shards, head_count, head_width * nstate)
+    summed = jnp.einsum(
+        "kh,khm->hm", weight, gathered.astype(jnp.float32), precision=precise
     )
-    return jnp.sum(weight[:, :, None, None] * gathered, axis=0)
+    return summed.reshape(head_count, head_width, nstate)
 
 
 def on_device(

time: 298 us -> 314 us (1.054)
  local copies, waits for them, and re-layouts: 4.92 us -> 16.9 us
  matrix products: 29.3 us -> 37.4 us
  other arithmetic: 9.51 us -> 5.09 us
    dot_general x0 -> x1, matrix products: none -> 8.01 us  [carried_state(): jnp.einsum('kh,khm->hm', weight, gathered.astype(jnp.float32), precision=...]
    reshape x0 -> x1, local copies, waits for them, and re-layouts: none -> 7.29 us  [carried_state(): everything[:, :rows, :].reshape(shards, head_count, head_width * nstate)]
    slice x0 -> x1, local copies, waits for them, and re-layouts: none -> 4.62 us  [carried_state(): everything[:, :rows, :].reshape(shards, head_count, head_width * nstate)]
    reduce_sum x1 -> x0, other arithmetic: 4.42 us -> none  [carried_state(): return jnp.sum(weight[:, :, None, None] * gathered, axis=0)]
  transfers between devices with their start and end apart: 7 -> 7, of which waited for: 5 -> 5; matrix products, arithmetic and copies ran while one was open for 7% -> 6% of each run, Pallas kernels for 0% -> 0%
where the time goes in v9:
time: 314 us; the launch traced here: 313 us
  waiting for transfers between devices  210 us (67%)
  matrix products  37.4 us (12%)
  blocking collectives  21.9 us (7%)
  local copies, waits for them, and re-layouts  16.9 us (5%)
  between operations  14.1 us (4%)
  starting transfers between devices  7.86 us (3%)
  other arithmetic  5.09 us (2%)
    reduce_scatter x1, waiting for transfers between devices, on_device(): summed = lax.psum_scatter(pair_sum, 'chip', scatter_dimension=0, tiled=True)  86.1 us
    all_gather x1, waiting for transfers between devices, on_device(): token_piece = lax.all_gather(chosen, 'chip', axis=0, tiled=True)  54.9 us
    all_gather x1, waiting for transfers between devices, carried_state(): everything = lax.all_gather(packed, CTX)  50.7 us
    all_to_all x1, blocking collectives, on_device(): arrived = lax.all_to_all(picked, 'exp', 0, 0)  21.9 us
    all_to_all x1, waiting for transfers between devices, on_device(): returned = lax.all_to_all(outgoing, 'exp', 0, 0)  13.1 us
    dot_general x1, matrix products, on_device(): jnp.dot(token_piece, gate_both, preferred_element_type=jnp.float32)  9.76 us
    dot_general x1, matrix products, on_device(): jnp.dot(hidden, down_both, preferred_element_type=jnp.float32)  8.94 us
    dot_general x1, matrix products, carried_state(): jnp.einsum('kh,khm->hm', weight, gathered.astype(jnp.float32), precision=...  8.01 us
  transfers between devices with their start and end apart: 7, of which 5 were waited for; matrix products, arithmetic and copies ran while one was open for 6% of the time, Pallas kernels for 0%

profile of v9, /device:TPU:2, one launch (start us, length us, event | category | flops | bytes accessed | tf_op | source)
XLA Modules:
  0.0 313.4 jit_solution(14742687712690972205)
XLA Ops:
  7.2 0.8 negate_multiply_fusion
  8.0 0.1 copy.40
  8.1 0.2 reduce_window_sum.22
  8.4 1.0 copy.43
  9.4 0.3 convolution_convert_fusion.2
  9.7 0.2 scatter.9
  9.9 0.7 pad_maximum_fusion
  10.5 0.0 all-gather.4.cloned.1.call-start
  10.6 0.1 copy.44
  10.7 1.0 convert_multiply_fusion.1
  11.7 0.1 copy.48
  11.8 0.7 fusion.50
  12.5 0.3 reduce_window_sum.23
  12.9 0.9 fusion.59
  13.8 50.7 %all-gather.6.cloned.1.call-done = bf16[16640,128]{1,0:T(8,128)(2,1)} async-done(((bf16[520,128]{1,0:T(8,128)(2,1)}), bf16[16640,128]{1,0:T(8,128)(2,1)}) %all-gather.6.cloned.1.call-update) | async-done | bytes 4259856 | tf_op jit(solution)/shard_map/all_gather | solution.py:49
  64.4 0.9 fusion.57
  65.4 4.6 %slice.54 = bf16[32,512,128]{2,1,0:T(8,128)(2,1)} slice(bf16[32,520,128]{2,1,0:T(8,128)(2,1)} %bitcast.63), slice={[0:32], [0:512], [0:128]} | slice | bytes 8388608 | tf_op jit(solution)/shard_map/slice | solution.py:60
  70.0 0.1 copy.55
  70.1 0.1 copy.56
  70.2 0.1 select_reduce_fusion
  70.3 0.1 select_bitcast_fusion
  70.4 0.1 copy.52
  70.4 7.3 %reshape.183 = bf16[32,8,8192]{2,1,0:T(8,128)(2,1)} reshape(bf16[32,512,128]{2,1,0:T(8,128)(2,1)} %slice.54) | data formatting | bytes 8388608 | tf_op jit(solution)/shard_map/reshape | solution.py:60
  77.7 8.0 %fusion.11 = f32[8,1,8192]{2,1,0:T(1,128)S(1)} fusion(f32[32,8,1]{0,2,1:T(1,128)S(1)} %copy.52, bf16[32,8,8192]{2,1,0:T(8,128)(2,1)} %reshape.183), kind=kOutput, calls=%fused_computation.12 | convolution fusion | flops 25165824 | bytes 4457472 | tf_op jit(solution)/shard_map/kh,khm->hm/dot_general | solution.py:61
  85.8 0.2 copy.69
  85.9 0.3 fusion.16
  86.2 0.8 multiply_reduce_fusion
  87.0 0.1 copy.49
  87.3 0.2 convolution_convert_fusion.1
  87.5 21.9 %all_to_all.10 = bf16[8,48,512]{2,1,0:T(8,128)(2,1)S(1)} all-to-all(bf16[8,48,512]{2,1,0:T(8,128)(2,1)S(1)} %convolution_convert_fusion.1), channel_id=1, replica_groups=mesh['chip'=16,'core'=2,'exp'=8] {'exp'}, dimensions={0} | all-to-all | bytes 786432 | tf_op jit(solution)/shard_map/all_to_all | solution.py:116
  109.4 0.1 convert_bitcast_fusion
  109.5 0.1 copy.58
  109.6 0.2 fusion.18
  109.8 0.9 multiply_convert_fusion.2
  110.7 0.0 reduce-scatter.2.cloned.1.call-start
  110.7 0.1 collective-permute-start
  110.8 0.5 collective-permute-start.1
  111.3 0.1 collective-permute-start.2
  111.4 5.4 %collective-permute-done = bf16[4096,384]{1,0:T(8,128)(2,1)} collective-permute-done((bf16[4096,384]{1,0:T(8,128)(2,1)}, bf16[4096,384]{1,0:T(8,128)(2,1)}, u32[]{:S(2)}, u32[]{:S(2)}) %collective-permute-start) | collective-permute-done | bytes 3145760 | tf_op jit(solution)/shard_map/ppermute | solution.py:129
  116.8 54.9 %all-gather.4.cloned.1.call-done = bf16[768,4096]{1,0:T(8,128)(2,1)} async-done(((bf16[48,4096]{1,0:T(8,128)(2,1)}), bf16[768,4096]{1,0:T(8,128)(2,1)}) %all-gather.4.cloned.1.call-update) | async-done | bytes 6291472 | tf_op jit(solution)/shard_map/all_gather | solution.py:132
  171.7 9.8 %fusion = f32[768,768]{1,0:T(8,128)S(1)} fusion(bf16[768,4096]{1,0:T(8,128)(2,1)} %all-gather.4.cloned.1.call-done, bf16[4096,384]{1,0:T(8,128)(2,1)} %collective-permute-done, bf16[4096,384]{1,0:T(8,128)(2,1)} %bitcast.73), kind=kOutput, calls=%fused_computation.1 | convolution fusion | flops 4844421120 | bytes 14942208 | tf_op jit(solution)/shard_map/dot_general | solution.py:137
  181.5 7.1 %fusion.4 = f32[768,768]{1,0:T(8,128)S(1)} fusion(bf16[768,4096]{1,0:T(8,128)(2,1)S(1)} %copy-done.8, bf16[4096,384]{1,0:T(8,128)(2,1)} %collective-permute-done.1, bf16[4096,384]{1,0:T(8,128)(2,1)S(1)} %bitcast.75), kind=kOutput, calls=%fused_computation.5 | convolution fusion | flops 4844421120 | bytes 14942208 | tf_op jit(solution)/shard_map/dot_general | solution.py:138
  188.7 8.9 %convolution_convert_fusion = bf16[768,4096]{1,0:T(8,128)(2,1)} fusion(bf16[384,4096]{1,0:T(8,128)(2,1)} %collective-permute-done.2, bf16[384,4096]{1,0:T(8,128)(2,1)S(1)} %bitcast.77, f32[768,768]{1,0:T(8,128)S(1)} %fusion.4, f32[768,768]{1,0:T(8,128)S(1)} %fusion), kind=kOutput, calls=%fused_computation | convolution fusion | flops 4851105792 | bytes 17301504 | tf_op jit(solution)/shard_map/dot_general | solution.py:140
  197.7 86.1 %reduce-scatter.2.cloned.1.call-done = bf16[48,4096]{1,0:T(8,128)(2,1)} async-done(((bf16[768,4096]{1,0:T(8,128)(2,1)}), bf16[48,4096]{1,0:T(8,128)(2,1)}) %reduce-scatter.2.cloned.1.call-update) | async-done | bytes 393232 | tf_op jit(solution)/shard_map/reduce_scatter | solution.py:141
  283.8 1.8 copy.68
  285.6 7.0 %all-to-all-start.1 = ((bf16[8,48,512]{2,1,0:T(8,128)(2,1)}), bf16[8,48,512]{2,1,0:T(8,128)(2,1)S(1)}, u32[]{:S(2)}, u32[]{:S(2)}) async-start(bf16[8,48,512]{2,1,0:T(8,128)(2,1)} %bitcast.60), calls=%async_computation.2 | async-start | bytes 786432 | tf_op jit(solution)/shard_map/all_to_all | solution.py:143
  292.7 13.1 %all-to-all-done.1 = bf16[8,48,512]{2,1,0:T(8,128)(2,1)S(1)} async-done(((bf16[8,48,512]{2,1,0:T(8,128)(2,1)}), bf16[8,48,512]{2,1,0:T(8,128)(2,1)S(1)}, u32[]{:S(2)}, u32[]{:S(2)}) %all-to-all-start.1) | async-done | bytes 393248 | tf_op jit(solution)/shard_map/all_to_all | solution.py:143
  305.7 1.1 fusion.17
  (45 shorter events, 0.4 us)
Async XLA Ops:
  7.2 2.3 copy-start
  7.2 57.3 %all-gather.6.cloned.1.call-start = ((), (), s32[]{:S(2)}) async-start(), calls=%async_computation.5 | async-start | bytes 4392960 | tf_op jit(solution)/shard_map/all_gather | solution.py:49
  10.5 161.2 %all-gather.4.cloned.1.call-start = ((), (), s32[]{:S(2)}) async-start(), calls=%async_computation.3 | async-start | bytes 6684672 | tf_op jit(solution)/shard_map/all_gather | solution.py:132
  77.7 8.2 %copy-start.2 = (bf16[128,128]{1,0:T(8,128)(2,1)S(1)}, bf16[128,128]{1,0:T(8,128)(2,1)}, u32[]{:S(2)}) copy-start(bf16[128,128]{1,0:T(8,128)(2,1)} %param.21) | copy-start | bytes 98308
  77.7 9.5 %copy-start.3 = (bf16[128,512]{1,0:T(8,128)(2,1)S(1)}, bf16[128,512]{1,0:T(8,128)(2,1)}, u32[]{:S(2)}) copy-start(bf16[128,512]{1,0:T(8,128)(2,1)} %param.25) | copy-start | bytes 393220
  77.7 9.5 %copy-start.6 = (f32[512]{0:T(512)S(1)}, f32[512]{0:T(512)}, u32[]{:S(2)}) copy-start(f32[512]{0:T(512)} %param.24) | copy-start | bytes 6148
  85.7 24.0 %copy-start.4 = (f32[4096]{0:T(1024)S(1)}, f32[4096]{0:T(1024)}, u32[]{:S(2)}) copy-start(f32[4096]{0:T(1024)} %param.26) | copy-start | bytes 49156
  87.2 94.2 %copy-start.1 = (bf16[128,512]{1,0:T(8,128)(2,1)}, bf16[128,512]{1,0:T(8,128)(2,1)S(1)}, u32[]{:S(2)}) copy-start(bf16[128,512]{1,0:T(8,128)(2,1)S(1)} %add_convert_fusion) | copy-start | bytes 393220
  110.7 173.1 %reduce-scatter.2.cloned.1.call-start = ((), (), s32[]{:S(2)}) async-start(), calls=%async_computation.4 | async-start | bytes 6684672 | tf_op jit(solution)/shard_map/reduce_scatter | solution.py:141
  110.7 6.1 %collective-permute-start = (bf16[4096,384]{1,0:T(8,128)(2,1)}, bf16[4096,384]{1,0:T(8,128)(2,1)}, u32[]{:S(2)}, u32[]{:S(2)}) collective-permute-start(bf16[4096,384]{1,0:T(8,128)(2,1)} %bitcast.72), channel_id=1, source_target_pairs={{0,8},{8,0},{1,9},{9,1},{2,10},{10,2},{3,11},{11,3},{4,12},{12,4},... | collective-permute-start | bytes 9437192 | tf_op jit(solution)/shard_map/ppermute | solution.py:129
  110.8 70.7 %collective-permute-start.1 = (bf16[4096,384]{1,0:T(8,128)(2,1)}, bf16[4096,384]{1,0:T(8,128)(2,1)}, u32[]{:S(2)}, u32[]{:S(2)}) collective-permute-start(bf16[4096,384]{1,0:T(8,128)(2,1)} %bitcast.74), channel_id=1, source_target_pairs={{0,8},{8,0},{1,9},{9,1},{2,10},{10,2},{3,11},{11,3},{4,12},{12,4},... | collective-permute-start | bytes 9437192 | tf_op jit(solution)/shard_map/ppermute | solution.py:130
  111.3 70.2 %copy-start.9 = (bf16[1,4096,384]{2,1,0:T(8,128)(2,1)S(1)}, bf16[1,4096,384]{2,1,0:T(8,128)(2,1)}, u32[]{:S(2)}) copy-start(bf16[1,4096,384]{2,1,0:T(8,128)(2,1)} %param.28) | copy-start | bytes 9437188
  111.3 77.3 %collective-permute-start.2 = (bf16[384,4096]{1,0:T(8,128)(2,1)}, bf16[384,4096]{1,0:T(8,128)(2,1)}, u32[]{:S(2)}, u32[]{:S(2)}) collective-permute-start(bf16[384,4096]{1,0:T(8,128)(2,1)} %bitcast.76), channel_id=1, source_target_pairs={{0,8},{8,0},{1,9},{9,1},{2,10},{10,2},{3,11},{11,3},{4,12},{12,4},... | collective-permute-start | bytes 9437192 | tf_op jit(solution)/shard_map/ppermute | solution.py:131
  171.7 9.8 %copy-start.8 = (bf16[768,4096]{1,0:T(8,128)(2,1)S(1)}, bf16[768,4096]{1,0:T(8,128)(2,1)}, u32[]{:S(2)}) copy-start(bf16[768,4096]{1,0:T(8,128)(2,1)} %all-gather.4.cloned.1.call-done) | copy-start | bytes 18874372
  181.5 7.2 %copy-start.10 = (bf16[1,384,4096]{2,1,0:T(8,128)(2,1)S(1)}, bf16[1,384,4096]{2,1,0:T(8,128)(2,1)}, u32[]{:S(2)}) copy-start(bf16[1,384,4096]{2,1,0:T(8,128)(2,1)} %param.29) | copy-start | bytes 9437188
  197.6 95.0 %copy-start.5 = (s32[128,2]{0,1:T(2,128)S(1)}, s32[128,2]{0,1:T(2,128)}, u32[]{:S(2)}) copy-start(s32[128,2]{0,1:T(2,128)} %param.30) | copy-start | bytes 3076
  197.6 95.0 %copy-start.7 = (f32[128,2]{0,1:T(2,128)S(1)}, f32[128,2]{0,1:T(2,128)}, u32[]{:S(2)}) copy-start(f32[128,2]{0,1:T(2,128)} %param.31) | copy-start | bytes 3076
  285.6 20.2 %all-to-all-start.1 = ((bf16[8,48,512]{2,1,0:T(8,128)(2,1)}), bf16[8,48,512]{2,1,0:T(8,128)(2,1)S(1)}, u32[]{:S(2)}, u32[]{:S(2)}) async-start(bf16[8,48,512]{2,1,0:T(8,128)(2,1)} %bitcast.60), calls=%async_computation.2 | async-start | bytes 786432 | tf_op jit(solution)/shard_map/all_to_all | solution.py:143
Sparse Core Ops, SparseCore 0:
  10.7 53.7 all-gather.5
  110.8 60.8 all-gather.3
  197.8 85.9 reduce-scatter.1
